TPU v7x, 512 devices: a whole 4x8x8 slice. The times are simulated.
512 devices in a mesh: tm: 32 (over x, y), space: 16 (over z, core).
Axes of the slice: x: 4, y: 8, z: 8, core: 2. Of those that a mesh axis runs over, the one named last changes fastest.
Arguments:
- data: bfloat16 [4096, 131072], P('tm', 'space'), may hold values from -40 to 40
- weights: float32 [131072], P('space'), may hold values from 1 to 30
- freqs: int32 [32], replicated, may hold values from 0 to 32, as said below
- n_keep: int32 [32], replicated, may hold values from 1 to 64, as said below
Outputs:
- mode_field: bfloat16 [32, 2, 64, 131072], P('tm', None, None, 'space')
- energy: float32 [32], P('tm')
Inputs may be any that keep to these rules, and one draw needn't show every extreme that they name: `freqs`: 32 distinct bins, among them 0 and 32, in an order drawn from the seed. `n_keep`: some frequency keeps all 64 columns and another keeps one.
All inputs are finite; a program needn't handle non-finite values.
Results may differ from a plain program's by a relative error of at most 0.0052.
Values may be sent and summed in bfloat16 or wider, within the bound.
No kernel may reach another device: no remote copies, remote signals or barrier semaphores. Data moves between devices by JAX's collectives and lax.ppermute only.
A program may use at most 64 MiB of HBM per device.

v0:
```python
import jax
import jax.numpy as jnp
from jax import lax
from jax.sharding import PartitionSpec as P

NT = 64
NS_STEPS = 4


def spectra_table(freqs):
    time_int = jnp.arange(NT, dtype=jnp.int32)
    time_float = time_int.astype(jnp.float32)
    window = 0.5 - 0.5 * jnp.cos(2.0 * jnp.pi * time_float / NT)
    norm = jnp.sqrt(jnp.sum(window * window))
    wrapped = freqs[:, None] * time_int[None, :] % NT
    phase_angle = 2.0 * jnp.pi * wrapped.astype(jnp.float32) / NT
    real_rows = window[None, :] * jnp.cos(phase_angle) / norm
    imag_rows = -window[None, :] * jnp.sin(phase_angle) / norm
    return jnp.concatenate([real_rows, imag_rows], axis=0).astype(jnp.bfloat16)


def transform_blocks(dft_table, snapshots, freq_count):
    block_count = snapshots.shape[0] // NT
    point_count = snapshots.shape[1]
    block_view = snapshots.reshape(block_count, NT, point_count)
    spectra = jnp.einsum("rt,btp->rbp", dft_table, block_view, preferred_element_type=jnp.float32)
    return spectra.reshape(2, freq_count, block_count, point_count)


def gram_terms(spectra, point_weights, total_points):
    spectra_re = spectra[0]
    spectra_im = spectra[1]
    stacked = jnp.concatenate([spectra_re, spectra_im], axis=1)
    square = (
        jnp.einsum(
            "fip,fjp->fij",
            stacked * point_weights[None, None, :],
            stacked,
            precision=lax.Precision.HIGHEST,
        )
        / total_points
    )
    return square


def unfold_terms(summed, block_count):
    g_one = summed[:, :block_count, :block_count] + summed[:, block_count:, block_count:]
    g_two = summed[:, :block_count, block_count:] - summed[:, block_count:, :block_count]
    return (g_one, g_two)


def inverse_root(embedded):
    size_two = embedded.shape[1]
    frobenius = jnp.sqrt(jnp.sum(embedded * embedded, axis=(1, 2)) + 1e-06)
    identity = jnp.broadcast_to(jnp.eye(size_two, dtype=jnp.float32), embedded.shape)
    current = embedded / frobenius[:, None, None]
    result = identity
    for sweep in range(NS_STEPS):
        factor = 1.5 * identity - 0.5 * jnp.einsum(
            "fij,fjk->fik", result, current, precision=lax.Precision.HIGHEST
        )
        current = jnp.einsum("fij,fjk->fik", current, factor, precision=lax.Precision.HIGHEST)
        result = jnp.einsum("fij,fjk->fik", factor, result, precision=lax.Precision.HIGHEST)
    return result


def finish_modes(spectra, summed, kept_counts, block_count):
    g_one, g_two = unfold_terms(summed, block_count)
    embedded = jnp.concatenate(
        [jnp.concatenate([g_one, -g_two], axis=2), jnp.concatenate([g_two, g_one], axis=2)], axis=1
    )
    inv_root = inverse_root(embedded)
    z_top = inv_root[:, :block_count, :block_count]
    z_low = inv_root[:, block_count:, :block_count]
    spectra_re = spectra[0]
    spectra_im = spectra[1]
    mode_re = jnp.einsum(
        "fij,fip->fjp", z_top, spectra_re, precision=lax.Precision.HIGHEST
    ) - jnp.einsum("fij,fip->fjp", z_low, spectra_im, precision=lax.Precision.HIGHEST)
    mode_im = jnp.einsum(
        "fij,fip->fjp", z_top, spectra_im, precision=lax.Precision.HIGHEST
    ) + jnp.einsum("fij,fip->fjp", z_low, spectra_re, precision=lax.Precision.HIGHEST)
    kept_mask = jnp.arange(block_count, dtype=jnp.int32)[None, :] < kept_counts[:, None]
    both_parts = jnp.stack([mode_re, mode_im], axis=1)
    mode_field = jnp.where(
        kept_mask[:, None, :, None], both_parts, jnp.zeros_like(both_parts)
    ).astype(jnp.bfloat16)
    energy = jnp.trace(g_one, axis1=1, axis2=2) / block_count
    return (mode_field, energy)


def shards(data, weights, freqs, n_keep):
    tm_count = lax.axis_size("tm")
    freq_count = freqs.shape[0]
    points_here = data.shape[1]
    total_points = points_here * lax.axis_size("space")
    block_count = data.shape[0] // NT * tm_count
    dft_table = spectra_table(freqs)
    spectra = transform_blocks(dft_table, data, freq_count)
    regrouped = lax.all_to_all(spectra, "tm", split_axis=1, concat_axis=2, tiled=True)
    partial_value = gram_terms(regrouped, weights, total_points)
    summed = lax.psum(partial_value, "space")
    kept_counts = lax.dynamic_slice_in_dim(n_keep, lax.axis_index("tm"), 1)
    mode_field, energy = finish_modes(regrouped, summed, kept_counts, block_count)
    return (mode_field, energy)


def solution(mesh):
    placed = (P("tm", "space"), P("space"), P(), P())
    return jax.shard_map(
        shards,
        mesh=mesh,
        in_specs=placed,
        out_specs=(P("tm", None, None, "space"), P("tm")),
        check_vma=False,
    )
```

profile of v0, /device:TPU:1, one launch (start us, length us, event | category | flops | bytes accessed | tf_op | source)
XLA Modules:
  0.0 300.4 jit_solution(1019790081844584022)
XLA Ops:
  7.2 0.0 copy-start
  7.2 0.7 multiply_reduce_fusion
  8.6 0.8 divide_convert_fusion.1
  9.4 0.0 copy-done
  9.4 0.7 fusion.36
  10.1 5.2 %copy.10 = f32[2,32,2,8192]{3,2,0,1:T(2,128)} copy(f32[2,32,2,8192]{3,1,2,0:T(8,128)S(1)} %fusion.36) | data formatting | bytes 8388608 | tf_op jit(solution)/shard_map/rt,btp->rbp/dot_general | solution.py:26
  15.3 0.0 copy-start.4
  15.3 10.7 %all-to-all-start = ((f32[2,32,2,8192]{3,2,0,1:T(2,128)}), f32[2,32,2,8192]{3,2,0,1:T(2,128)}, u32[]{:S(2)}, u32[]{:S(2)}) async-start(f32[2,32,2,8192]{3,2,0,1:T(2,128)} %copy.10), calls=%async_computation | async-start | bytes 8388608 | tf_op jit(solution)/shard_map/all_to_all | solution.py:100
  26.1 0.0 all-reduce.2.cloned.1.call-start
  26.1 0.0 copy-done.4
  26.1 0.6 dynamic_slice.3
  26.7 92.0 %all-to-all-done = f32[2,32,2,8192]{3,2,0,1:T(2,128)} async-done(((f32[2,32,2,8192]{3,2,0,1:T(2,128)}), f32[2,32,2,8192]{3,2,0,1:T(2,128)}, u32[]{:S(2)}, u32[]{:S(2)}) %all-to-all-start) | async-done | bytes 4194336 | tf_op jit(solution)/shard_map/all_to_all | solution.py:100
  118.7 4.8 %fusion.35 = (f32[1,32,2,8192]{3,2,0,1:T(2,128)}, f32[1,32,2,8192]{3,2,0,1:T(2,128)}) fusion(f32[2,32,2,8192]{3,2,0,1:T(2,128)} %all-to-all-done), kind=kLoop, calls=%fused_computation.61 | loop fusion | bytes 8388608 | tf_op jit(solution)/shard_map/slice | solution.py:31
  123.5 5.2 %squeeze.8 = f32[1,64,8192]{2,0,1:T(1,128)} reshape(f32[1,32,2,8192]{3,2,0,1:T(2,128)} %get-tuple-element.6) | data formatting | bytes 4194304 | tf_op jit(solution)/shard_map/squeeze | solution.py:31
  128.7 3.7 %concatenate.53 = f32[64,8192]{1,0:T(8,128)} reshape(f32[1,32,2,8192]{3,2,0,1:T(2,128)} %get-tuple-element.6) | data formatting | bytes 4194304 | tf_op jit(solution)/shard_map/concatenate | solution.py:33
  132.4 5.2 %squeeze.9 = f32[1,64,8192]{2,0,1:T(1,128)} reshape(f32[1,32,2,8192]{3,2,0,1:T(2,128)} %get-tuple-element.7) | data formatting | bytes 4194304 | tf_op jit(solution)/shard_map/squeeze | solution.py:32
  137.6 3.6 %concatenate.54 = f32[64,8192]{1,0:T(8,128)} reshape(f32[1,32,2,8192]{3,2,0,1:T(2,128)} %get-tuple-element.7) | data formatting | bytes 4194304 | tf_op jit(solution)/shard_map/concatenate | solution.py:33
  141.3 0.0 copy-start.3
  141.3 12.4 %pad_maximum_fusion = f32[1,128,8192]{2,0,1:T(1,128)} fusion(f32[1,64,8192]{2,0,1:T(1,128)} %squeeze.9, f32[1,64,8192]{2,0,1:T(1,128)} %squeeze.8), kind=kLoop, calls=%fused_computation.8 | loop fusion | flops 1048576 | bytes 8388608 | tf_op jit(solution)/shard_map/concatenate | solution.py:33
  153.6 0.0 copy-done.3
  153.6 9.6 %fusion.16 = f32[1,128,128]{2,1,0:T(8,128)} fusion(f32[1,128,8192]{2,0,1:T(1,128)} %pad_maximum_fusion, f32[64,8192]{1,0:T(8,128)} %concatenate.54, f32[64,8192]{1,0:T(8,128)} %concatenate.53, f32[8192]{0:T(1024)S(1)} %copy-done.3), kind=kOutput, calls=%fused_computation.24 | convolution fusion | flops 1612726272 | bytes 8486912 | tf_op jit(solution)/shard_map/fip,fjp->fij/dot_general | solution.py:35
  163.2 0.0 all-reduce.2.cloned.1.call-update
  163.3 0.7 iota_compare_fusion.4
  163.9 110.4 %all-reduce.2.cloned.1.call-done = f32[1,128,128]{2,1,0:T(8,128)} async-done(((f32[1,128,128]{2,1,0:T(8,128)}), f32[1,128,128]{2,1,0:T(8,128)}) %all-reduce.2.cloned.1.call-update) | async-done | bytes 65552 | tf_op jit(solution)/shard_map/psum | solution.py:102
  274.3 1.5 fusion.34
  275.9 0.7 fusion.19
  276.6 0.1 maximum_bitcast_fusion
  277.3 0.0 copy-start.1
  277.3 0.2 fusion.12
  277.5 0.2 fusion.29
  277.7 0.2 fusion.20
  277.9 0.2 fusion.11
  278.1 0.2 fusion.38
  278.3 0.2 fusion.37
  278.6 0.2 fusion.10
  278.8 0.2 fusion.40
  279.0 0.2 fusion.39
  279.2 0.2 fusion.9
  279.4 0.2 convolution_bitcast_fusion
  279.6 0.0 copy-done.1
  279.6 0.0 copy-start.2
  279.6 2.2 fusion.22
  281.8 0.0 copy-done.2
  281.8 1.9 fusion.21
  283.7 2.0 fusion.1
  285.8 3.0 %fusion = bf16[1,1,64,8192]{3,2,1,0:T(8,128)(2,1)} fusion(f32[64,8192]{1,0:T(8,128)S(1)} %fusion.21, f32[64,8192]{1,0:T(8,128)S(1)} %copy-done.1, f32[1,128,128]{2,1,0:T(8,128)S(1)} %convolution_bitcast_fusion), kind=kOutput, calls=%fused_computation.1 | convolution fusion | flops 403701760 | bytes 5275648 | tf_op jit(solution)/shard_map/fij,fip->fjp/dot_general | solution.py:82
  289.4 3.0 fusion.5
  (2 shorter events, 0.1 us)
Async XLA Ops:
  7.2 2.2 copy-start
  15.3 10.8 %copy-start.4 = (s32[32]{0:T(128)S(1)}, s32[32]{0:T(128)}, u32[]{:S(2)}) copy-start(s32[32]{0:T(128)} %param.7) | copy-start | bytes 388
  15.3 103.4 %all-to-all-start = ((f32[2,32,2,8192]{3,2,0,1:T(2,128)}), f32[2,32,2,8192]{3,2,0,1:T(2,128)}, u32[]{:S(2)}, u32[]{:S(2)}) async-start(f32[2,32,2,8192]{3,2,0,1:T(2,128)} %copy.10), calls=%async_computation | async-start | bytes 8388608 | tf_op jit(solution)/shard_map/all_to_all | solution.py:100
  26.1 248.3 %all-reduce.2.cloned.1.call-start = ((), (), s32[]{:S(2)}) async-start(), calls=%async_computation.1 | async-start | bytes 131072 | tf_op jit(solution)/shard_map/psum | solution.py:102
  141.3 12.4 %copy-start.3 = (f32[8192]{0:T(1024)S(1)}, f32[8192]{0:T(1024)}, u32[]{:S(2)}) copy-start(f32[8192]{0:T(1024)} %param.5) | copy-start | bytes 98308
  277.3 2.3 copy-start.1
  279.6 2.2 copy-start.2
Sparse Core Ops, SparseCore 0:
  163.4 110.9 all-reduce.1
where the time goes:
time: 301 us; the launch traced here: 300 us
  waiting for transfers between devices  202 us (67%)
  local copies, waits for them, and re-layouts  28.4 us (9%)
  matrix products  21.6 us (7%)
  other arithmetic  19.8 us (7%)
  between operations  17.4 us (6%)
  starting transfers between devices  10.8 us (4%)
    psum x1, waiting for transfers between devices, shards(): summed = lax.psum(partial_value, 'space')  110 us
    all_to_all x1, waiting for transfers between devices, shards(): lax.all_to_all(spectra, 'tm', split_axis=1, concat_axis=2, tiled=True)  92 us
    concatenate x1, other arithmetic, gram_terms(): stacked = jnp.concatenate([spectra_re, spectra_im], axis=1)  12.4 us
    all_to_all x1, starting transfers between devices, shards(): lax.all_to_all(spectra, 'tm', split_axis=1, concat_axis=2, tiled=True)  10.7 us
    dot_general x1, matrix products, gram_terms(): jnp.einsum('fip,fjp->fij', stacked * point_weights[None, None, :], stacke...  9.63 us
    concatenate x2, local copies, waits for them, and re-layouts, gram_terms(): stacked = jnp.concatenate([spectra_re, spectra_im], axis=1)  7.32 us
  transfers between devices with their start and end apart: 2, of which 2 were waited for; matrix products, arithmetic and copies ran while one was open for 0% of the time, Pallas kernels for 0%

commit v1 on v0

v1 whole, which is shorter than its diff:
```python
import jax
import jax.numpy as jnp
from jax import lax
from jax.sharding import PartitionSpec as P

NT = 64
NS_STEPS = 4
HIGH = lax.Precision.HIGHEST


def spectra_table(freqs):
    time_int = jnp.arange(NT, dtype=jnp.int32)
    time_float = time_int.astype(jnp.float32)
    window = 0.5 - 0.5 * jnp.cos(2.0 * jnp.pi * time_float / NT)
    norm = jnp.sqrt(jnp.sum(window * window))
    wrapped = freqs[:, None] * time_int[None, :] % NT
    phase_angle = 2.0 * jnp.pi * wrapped.astype(jnp.float32) / NT
    real_rows = window[None, :] * jnp.cos(phase_angle) / norm
    imag_rows = -window[None, :] * jnp.sin(phase_angle) / norm
    return jnp.concatenate([real_rows, imag_rows], axis=0).astype(jnp.bfloat16)


def transform_blocks(dft_table, snapshots, freq_count):
    local_blocks = snapshots.shape[0] // NT
    point_count = snapshots.shape[1]
    block_view = snapshots.reshape(local_blocks, NT, point_count)
    table_view = dft_table.reshape(2, freq_count, NT)
    return jnp.einsum(
        "rft,btp->frbp", table_view, block_view, preferred_element_type=jnp.float32
    )


def butterfly_sum(value, axis, size):
    step = 1
    while step < size:
        pairs = [(i, i ^ step) for i in range(size)]
        value = value + lax.ppermute(value, axis, pairs)
        step *= 2
    return value


def inverse_root(embedded):
    size_two = embedded.shape[0]
    frobenius = jnp.sqrt(jnp.sum(embedded * embedded) + 1e-06)
    identity = jnp.eye(size_two, dtype=jnp.float32)
    current = embedded / frobenius
    result = identity
    for sweep in range(NS_STEPS):
        factor = 1.5 * identity - 0.5 * jnp.dot(result, current, precision=HIGH)
        current = jnp.dot(current, factor, precision=HIGH)
        result = jnp.dot(factor, result, precision=HIGH)
    return result


def shards(data, weights, freqs, n_keep):
    tm_count = lax.axis_size("tm")
    space_count = lax.axis_size("space")
    freq_count = freqs.shape[0]
    points_here = data.shape[1]
    total_points = points_here * space_count
    local_blocks = data.shape[0] // NT
    block_count = local_blocks * tm_count
    rows = 2 * block_count

    dft_table = spectra_table(freqs)
    spectra = transform_blocks(dft_table, data, freq_count)
    gathered = lax.all_to_all(spectra, "tm", split_axis=0, concat_axis=0, tiled=True)
    stacked = gathered.reshape(rows, points_here)

    square = jnp.dot(stacked * weights[None, :], stacked.T, precision=HIGH) / total_points
    square = square.reshape(tm_count, 2, local_blocks, tm_count, 2, local_blocks)
    square = square.transpose(1, 0, 2, 4, 3, 5).reshape(rows, rows)
    g_one = square[:block_count, :block_count] + square[block_count:, block_count:]
    g_two = square[:block_count, block_count:] - square[block_count:, :block_count]
    summed = butterfly_sum(jnp.stack([g_one, g_two]), "space", space_count)
    g_one = summed[0]
    g_two = summed[1]

    embedded = jnp.concatenate(
        [jnp.concatenate([g_one, -g_two], axis=1), jnp.concatenate([g_two, g_one], axis=1)], axis=0
    )
    inv_root = inverse_root(embedded)
    z_top = inv_root[:block_count, :block_count]
    z_low = inv_root[block_count:, :block_count]
    coeff = jnp.concatenate(
        [jnp.concatenate([z_top.T, -z_low.T], axis=1), jnp.concatenate([z_low.T, z_top.T], axis=1)],
        axis=0,
    )
    coeff = coeff.reshape(rows, 2, tm_count, local_blocks).transpose(0, 2, 1, 3).reshape(rows, rows)
    modes = jnp.dot(coeff, stacked, precision=HIGH).reshape(1, 2, block_count, points_here)

    kept_count = lax.dynamic_slice_in_dim(n_keep, lax.axis_index("tm"), 1)
    kept_mask = jnp.arange(block_count, dtype=jnp.int32)[None, None, :, None] < kept_count[:, None, None, None]
    mode_field = jnp.where(kept_mask, modes, jnp.zeros_like(modes)).astype(jnp.bfloat16)
    energy = (jnp.trace(g_one) / block_count).reshape(1)
    return (mode_field, energy)


def solution(mesh):
    placed = (P("tm", "space"), P("space"), P(), P())
    return jax.shard_map(
        shards,
        mesh=mesh,
        in_specs=placed,
        out_specs=(P("tm", None, None, "space"), P("tm")),
        check_vma=False,
    )
```

time: 301 us -> 203 us (0.67)
  waiting for transfers between devices: 202 us -> 4.02 us
  blocking collectives: 0 us -> 102 us
  starting transfers between devices: 10.8 us -> 25.2 us
  between operations: 17.4 us -> 4.07 us
  local copies, waits for them, and re-layouts: 28.4 us -> 40.9 us
  other arithmetic: 19.8 us -> 7.44 us
  matrix products: 21.6 us -> 17.6 us
    psum x1 -> x0, waiting for transfers between devices: 110 us -> none  [shards(): summed = lax.psum(partial_value, 'space')]
    all_to_all x0 -> x1, blocking collectives: none -> 102 us  [shards(): lax.all_to_all(spectra, 'tm', split_axis=0, concat_axis=0, tiled=True)]
    all_to_all x1 -> x0, waiting for transfers between devices: 92 us -> none  [shards(): lax.all_to_all(spectra, 'tm', split_axis=1, concat_axis=2, tiled=True)]
    ppermute x0 -> x4, starting transfers between devices: none -> 25.2 us  [butterfly_sum(): value = value + lax.ppermute(value, axis, pairs)]
    reshape x0 -> x4, local copies, waits for them, and re-layouts: none -> 23.9 us  [the longest x2 12.1 us: shards(): stacked = gathered.reshape(rows, points_here)]
    concatenate x2 -> x1, other arithmetic: 12.4 us -> 0.09 us  [shards(): jnp.concatenate([jnp.concatenate([z_top.T, -z_low.T], axis=1), jnp.concat...]
    all_to_all x1 -> x0, starting transfers between devices: 10.7 us -> none  [shards(): lax.all_to_all(spectra, 'tm', split_axis=1, concat_axis=2, tiled=True)]
    squeeze x2 -> x1, local copies, waits for them, and re-layouts: 10.5 us -> 0.01 us  [shards(): g_two = summed[1]]
  transfers between devices with their start and end apart: 2 -> 4, of which waited for: 2 -> 3; matrix products, arithmetic and copies ran while one was open for 0% -> 4% of each run, Pallas kernels for 0% -> 0%
where the time goes in v1:
time: 203 us; the launch traced here: 201 us
  blocking collectives  102 us (50%)
  local copies, waits for them, and re-layouts  40.9 us (20%)
  starting transfers between devices  25.2 us (12%)
  matrix products  17.6 us (9%)
  other arithmetic  7.44 us (4%)
  between operations  4.07 us (2%)
  waiting for transfers between devices  4.02 us (2%)
    all_to_all x1, blocking collectives, shards(): lax.all_to_all(spectra, 'tm', split_axis=0, concat_axis=0, tiled=True)  102 us
    ppermute x4, starting transfers between devices, butterfly_sum(): value = value + lax.ppermute(value, axis, pairs)  25.2 us
    reshape x2, local copies, waits for them, and re-layouts, shards(): stacked = gathered.reshape(rows, points_here)  12.1 us
    reshape x1, local copies, waits for them, and re-layouts, shards(): square.reshape(tm_count, 2, local_blocks, tm_count, 2, local_blocks)  7.79 us
    dot_general x1, matrix products, shards(): jnp.dot(coeff, stacked, precision=HIGH)  7.55 us
    dot_general x1, matrix products, shards(): jnp.dot(stacked * weights[None, :], stacked.T, precision=HIGH)  6.95 us
    mul x1, local copies, waits for them, and re-layouts, shards(): stacked * weights[None, :]  6.08 us
    transpose x1, local copies, waits for them, and re-layouts, shards(): square = square.transpose(1, 0, 2, 4, 3, 5).reshape(rows, rows)  4.74 us
  transfers between devices with their start and end apart: 4, of which 3 were waited for; matrix products, arithmetic and copies ran while one was open for 4% of the time, Pallas kernels for 0%

profile of v1, /device:TPU:1, one launch (start us, length us, event | category | flops | bytes accessed | tf_op | source)
XLA Modules:
  0.0 201.3 jit_solution(240627350875779938)
XLA Ops:
  0.6 0.0 copy-start
  0.7 0.7 multiply_reduce_fusion.1
  2.0 0.8 divide_convert_fusion.1
  2.9 0.0 copy-done
  2.9 0.7 convolution_bitcast_fusion
  3.6 3.2 %copy.13 = f32[32,2,2,8192]{3,2,1,0:T(2,128)S(1)} copy(f32[32,2,2,8192]{3,0,2,1:T(8,128)S(1)} %convolution_bitcast_fusion) | data formatting | bytes 8388608 | tf_op jit(solution)/shard_map/rft,btp->frbp/transpose | solution.py:28
  6.8 0.0 copy-start.2
  6.8 102.2 %all_to_all.5 = f32[32,2,2,8192]{3,2,1,0:T(2,128)S(1)} all-to-all(f32[32,2,2,8192]{3,2,1,0:T(2,128)S(1)} %copy.13), channel_id=1, replica_groups=mesh['tm'=32,'space'=16] {'tm'}, dimensions={0} | all-to-all | bytes 8388608 | tf_op jit(solution)/shard_map/all_to_all | solution.py:67
  109.0 1.9 copy-done.1
  110.9 0.0 copy-done.2
  110.9 3.7 %broadcast_multiply_fusion = f32[32,2,2,8192]{3,2,1,0:T(2,128)} fusion(f32[32,2,2,8192]{3,2,1,0:T(2,128)S(1)} %all_to_all.5, f32[8192]{0:T(1024)S(1)} %copy-done.2), kind=kLoop, calls=%fused_computation.4 | loop fusion | flops 1048576 | bytes 8421376 | tf_op jit(solution)/shard_map/mul | solution.py:70
  114.6 6.1 %mul.102 = f32[128,8192]{1,0:T(8,128)} reshape(f32[32,2,2,8192]{3,2,1,0:T(2,128)} %broadcast_multiply_fusion) | data formatting | bytes 8388608 | tf_op jit(solution)/shard_map/mul | solution.py:70
  120.7 6.1 %reshape.69 = f32[128,8192]{1,0:T(8,128)} reshape(f32[32,2,2,8192]{3,2,1,0:T(2,128)} %copy-done.1) | data formatting | bytes 8388608 | tf_op jit(solution)/shard_map/reshape | solution.py:68
  126.7 6.9 %convolution_multiply_fusion.4 = f32[128,128]{1,0:T(8,128)S(1)} fusion(f32[128,8192]{1,0:T(8,128)} %mul.102, f32[128,8192]{1,0:T(8,128)} %reshape.69), kind=kOutput, calls=%fused_computation.13 | convolution fusion | flops 1610629120 | bytes 8454144 | tf_op jit(solution)/shard_map/dot_general | solution.py:70
  133.7 7.8 %reshape.70 = f32[32,2,2,32,2,2]{5,4,3,2,1,0:T(2,128)} reshape(f32[128,128]{1,0:T(8,128)S(1)} %convolution_multiply_fusion.4) | data formatting | bytes 131072 | tf_op jit(solution)/shard_map/reshape | solution.py:71
  141.5 4.7 %copy.14 = f32[2,32,2,2,32,2]{5,4,3,2,1,0:T(8,128)} copy(f32[2,32,2,2,32,2]{5,3,4,2,0,1:T(2,128)} %bitcast.64) | data formatting | bytes 131072 | tf_op jit(solution)/shard_map/transpose | solution.py:72
  146.2 4.0 %reshape.71 = f32[128,128]{1,0:T(8,128)S(1)} reshape(f32[2,32,2,2,32,2]{5,4,3,2,1,0:T(8,128)} %copy.14) | data formatting | bytes 131072 | tf_op jit(solution)/shard_map/reshape | solution.py:72
  150.2 0.1 fusion.9
  150.3 7.1 %collective-permute-start = (f32[2,64,64]{2,1,0:T(8,128)S(1)}, f32[2,64,64]{2,1,0:T(8,128)S(1)}, u32[]{:S(2)}, u32[]{:S(2)}) collective-permute-start(f32[2,64,64]{2,1,0:T(8,128)S(1)} %pad_maximum_fusion), channel_id=1, source_target_pairs={{0,1},{1,0},{2,3},{3,2},{4,5},{5,4},{6,7},{7,6},{8,9},{9,8},{10,11... | collective-permute-start | bytes 98312 | tf_op jit(solution)/shard_map/ppermute | solution.py:37
  157.5 0.9 collective-permute-done
  158.4 4.0 %collective-permute-start.1 = (f32[2,64,64]{2,1,0:T(8,128)S(1)}, f32[2,64,64]{2,1,0:T(8,128)S(1)}, u32[]{:S(2)}, u32[]{:S(2)}) collective-permute-start(f32[2,64,64]{2,1,0:T(8,128)S(1)} %fusion.20), channel_id=1, source_target_pairs={{0,2},{1,3},{2,0},{3,1},{4,6},{5,7},{6,4},{7,5},{8,10},{9,11},{10,... | collective-permute-start | bytes 98312 | tf_op jit(solution)/shard_map/ppermute | solution.py:37
  162.4 2.1 %collective-permute-done.1 = f32[2,64,64]{2,1,0:T(8,128)S(1)} collective-permute-done((f32[2,64,64]{2,1,0:T(8,128)S(1)}, f32[2,64,64]{2,1,0:T(8,128)S(1)}, u32[]{:S(2)}, u32[]{:S(2)}) %collective-permute-start.1) | collective-permute-done | bytes 32800 | tf_op jit(solution)/shard_map/ppermute | solution.py:37
  164.5 5.8 %collective-permute-start.2 = (f32[2,64,64]{2,1,0:T(8,128)S(1)}, f32[2,64,64]{2,1,0:T(8,128)S(1)}, u32[]{:S(2)}, u32[]{:S(2)}) collective-permute-start(f32[2,64,64]{2,1,0:T(8,128)S(1)} %fusion.49), channel_id=1, source_target_pairs={{0,4},{1,5},{2,6},{3,7},{4,0},{5,1},{6,2},{7,3},{8,12},{9,13},{10,... | collective-permute-start | bytes 98312 | tf_op jit(solution)/shard_map/ppermute | solution.py:37
  170.3 0.6 dynamic_slice.3
  170.9 1.0 collective-permute-done.2
  172.0 8.2 %collective-permute-start.3 = (f32[2,64,64]{2,1,0:T(8,128)S(1)}, f32[2,64,64]{2,1,0:T(8,128)S(1)}, u32[]{:S(2)}, u32[]{:S(2)}) collective-permute-start(f32[2,64,64]{2,1,0:T(8,128)S(1)} %add.32), channel_id=1, source_target_pairs={{0,8},{1,9},{2,10},{3,11},{4,12},{5,13},{6,14},{7,15},{8,0},{9,1},... | collective-permute-start | bytes 98312 | tf_op jit(solution)/shard_map/ppermute | solution.py:37
  180.2 0.7 iota_compare_fusion.4
  180.8 6.1 %reshape.76 = f32[128,8192,1]{1,0,2:T(8,128)} reshape(f32[32,2,2,8192]{3,2,1,0:T(2,128)} %copy-done.1) | data formatting | bytes 8388608 | tf_op jit(solution)/shard_map/reshape | solution.py:68
  186.9 0.0 collective-permute-done.3
  187.0 0.6 select_reduce_fusion
  187.6 0.7 multiply_reduce_fusion
  189.0 0.3 fusion.5
  189.2 0.3 fusion.10
  189.5 0.2 fusion.7
  189.7 0.2 fusion.4
  189.9 0.2 fusion.22
  190.1 0.2 fusion.21
  190.3 0.2 fusion.3
  190.5 0.2 fusion.24
  190.7 0.2 fusion.23
  190.9 0.2 fusion.2
  191.2 0.3 fusion.25
  191.5 0.1 slice_bitcast_fusion
  191.5 0.1 fusion.19
  191.6 0.1 maximum_maximum_fusion.1
  191.7 0.1 copy.15
  191.8 0.1 dot_general.57
  192.6 7.5 %fusion.1 = bf16[1,2,64,8192]{3,2,1,0:T(8,128)(2,1)} fusion(f32[128,8192,1]{1,0,2:T(8,128)} %reshape.76, pred[64]{0:T(512)(128)(4,1)S(1)} %iota_compare_fusion.4, f32[2,64,128]{1,0,2:T(2,128)S(1)} %dot_general.57), kind=kOutput, calls=%fused_computation.3 | convolution fusion | flops 1612709888 | bytes 6357056 | tf_op jit(solution)/shard_map/dot_general | solution.py:90
  (12 shorter events, 0.1 us)
Async XLA Ops:
  0.6 2.2 %copy-start = (bf16[128,8192]{1,0:T(8,128)(2,1)S(1)}, bf16[128,8192]{1,0:T(8,128)(2,1)}, u32[]{:S(2)}) copy-start(bf16[128,8192]{1,0:T(8,128)(2,1)} %param.4) | copy-start | bytes 6291460
  6.8 104.1 %copy-start.2 = (f32[8192]{0:T(1024)S(1)}, f32[8192]{0:T(1024)}, u32[]{:S(2)}) copy-start(f32[8192]{0:T(1024)} %param.5) | copy-start | bytes 98308
  109.0 1.9 copy-start.1
  146.2 24.1 %copy-start.3 = (s32[32]{0:T(128)S(1)}, s32[32]{0:T(128)}, u32[]{:S(2)}) copy-start(s32[32]{0:T(128)} %param.7) | copy-start | bytes 388
  150.3 8.0 %collective-permute-start = (f32[2,64,64]{2,1,0:T(8,128)S(1)}, f32[2,64,64]{2,1,0:T(8,128)S(1)}, u32[]{:S(2)}, u32[]{:S(2)}) collective-permute-start(f32[2,64,64]{2,1,0:T(8,128)S(1)} %pad_maximum_fusion), channel_id=1, source_target_pairs={{0,1},{1,0},{2,3},{3,2},{4,5},{5,4},{6,7},{7,6},{8,9},{9,8},{10,11... | collective-permute-start | bytes 98312 | tf_op jit(solution)/shard_map/ppermute | solution.py:37
  158.4 6.1 %collective-permute-start.1 = (f32[2,64,64]{2,1,0:T(8,128)S(1)}, f32[2,64,64]{2,1,0:T(8,128)S(1)}, u32[]{:S(2)}, u32[]{:S(2)}) collective-permute-start(f32[2,64,64]{2,1,0:T(8,128)S(1)} %fusion.20), channel_id=1, source_target_pairs={{0,2},{1,3},{2,0},{3,1},{4,6},{5,7},{6,4},{7,5},{8,10},{9,11},{10,... | collective-permute-start | bytes 98312 | tf_op jit(solution)/shard_map/ppermute | solution.py:37
  164.5 7.5 %collective-permute-start.2 = (f32[2,64,64]{2,1,0:T(8,128)S(1)}, f32[2,64,64]{2,1,0:T(8,128)S(1)}, u32[]{:S(2)}, u32[]{:S(2)}) collective-permute-start(f32[2,64,64]{2,1,0:T(8,128)S(1)} %fusion.49), channel_id=1, source_target_pairs={{0,4},{1,5},{2,6},{3,7},{4,0},{5,1},{6,2},{7,3},{8,12},{9,13},{10,... | collective-permute-start | bytes 98312 | tf_op jit(solution)/shard_map/ppermute | solution.py:37
  172.0 15.0 %collective-permute-start.3 = (f32[2,64,64]{2,1,0:T(8,128)S(1)}, f32[2,64,64]{2,1,0:T(8,128)S(1)}, u32[]{:S(2)}, u32[]{:S(2)}) collective-permute-start(f32[2,64,64]{2,1,0:T(8,128)S(1)} %add.32), channel_id=1, source_target_pairs={{0,8},{1,9},{2,10},{3,11},{4,12},{5,13},{6,14},{7,15},{8,0},{9,1},... | collective-permute-start | bytes 98312 | tf_op jit(solution)/shard_map/ppermute | solution.py:37

commit v2 on v1

--- a/solution.py
+++ b/solution.py
@@ -6,6 +6,8 @@
 NT = 64
 NS_STEPS = 4
 HIGH = lax.Precision.HIGHEST
+THREE_PASS = lax.Precision.HIGH
+LINK_SCALE = 128.0
 
 
 def spectra_table(freqs):
@@ -64,10 +66,11 @@
 
     dft_table = spectra_table(freqs)
     spectra = transform_blocks(dft_table, data, freq_count)
-    gathered = lax.all_to_all(spectra, "tm", split_axis=0, concat_axis=0, tiled=True)
-    stacked = gathered.reshape(rows, points_here)
+    sent = (spectra * LINK_SCALE).astype(jnp.float16)
+    gathered = lax.all_to_all(sent, "tm", split_axis=0, concat_axis=0, tiled=True)
+    stacked = gathered.reshape(rows, points_here).astype(jnp.float32) * (1.0 / LINK_SCALE)
 
-    square = jnp.dot(stacked * weights[None, :], stacked.T, precision=HIGH) / total_points
+    square = jnp.dot(stacked * weights[None, :], stacked.T, precision=THREE_PASS) / total_points
     square = square.reshape(tm_count, 2, local_blocks, tm_count, 2, local_blocks)
     square = square.transpose(1, 0, 2, 4, 3, 5).reshape(rows, rows)
     g_one = square[:block_count, :block_count] + square[block_count:, block_count:]
@@ -87,7 +90,7 @@
         axis=0,
     )
     coeff = coeff.reshape(rows, 2, tm_count, local_blocks).transpose(0, 2, 1, 3).reshape(rows, rows)
-    modes = jnp.dot(coeff, stacked, precision=HIGH).reshape(1, 2, block_count, points_here)
+    modes = jnp.dot(coeff, stacked, precision=THREE_PASS).reshape(1, 2, block_count, points_here)
 
     kept_count = lax.dynamic_slice_in_dim(n_keep, lax.axis_index("tm"), 1)
     kept_mask = jnp.arange(block_count, dtype=jnp.int32)[None, None, :, None] < kept_count[:, None, None, None]

time: 203 us -> 159 us (0.78)
  blocking collectives: 102 us -> 0 us
  waiting for transfers between devices: 4.02 us -> 52.7 us
  starting transfers between devices: 25.2 us -> 32.8 us
  other arithmetic: 7.44 us -> 13.2 us
  matrix products: 17.6 us -> 14.1 us
    all_to_all x1 -> x0, blocking collectives: 102 us -> none  [shards(): lax.all_to_all(spectra, 'tm', split_axis=0, concat_axis=0, tiled=True)]
    all_to_all x0 -> x1, waiting for transfers between devices: none -> 48.7 us  [shards(): lax.all_to_all(sent, 'tm', split_axis=0, concat_axis=0, tiled=True)]
    reshape x2 -> x0, local copies, waits for them, and re-layouts: 12.1 us -> none  [shards(): stacked = gathered.reshape(rows, points_here)]
    mul x0 -> x2, local copies, waits for them, and re-layouts: none -> 12.1 us  [shards(): gathered.reshape(rows, points_here).astype(jnp.float32) * (1.0 / LINK_SCALE)]
    all_to_all x0 -> x1, starting transfers between devices: none -> 10.8 us  [shards(): lax.all_to_all(sent, 'tm', split_axis=0, concat_axis=0, tiled=True)]
    mul x1 -> x2, other arithmetic: 3.67 us -> 9.45 us  [shards(): stacked * weights[None, :]]
    convert_element_type x0 -> x1, local copies, waits for them, and re-layouts: none -> 4.17 us  [shards(): sent = (spectra * LINK_SCALE).astype(jnp.float16)]
    dot_general x2, matrix products: 14.5 us -> 11 us  [the longest x1 5.59 us: shards(): jnp.dot(coeff, stacked, precision=THREE_PASS)]
  transfers between devices with their start and end apart: 4 -> 5, of which waited for: 3 -> 4; matrix products, arithmetic and copies ran while one was open for 4% -> 5% of each run, Pallas kernels for 0% -> 0%
where the time goes in v2:
time: 159 us; the launch traced here: 157 us
  waiting for transfers between devices  52.7 us (33%)
  local copies, waits for them, and re-layouts  39.9 us (25%)
  starting transfers between devices  32.8 us (21%)
  matrix products  14.1 us (9%)
  other arithmetic  13.2 us (8%)
  between operations  4.09 us (3%)
    all_to_all x1, waiting for transfers between devices, shards(): lax.all_to_all(sent, 'tm', split_axis=0, concat_axis=0, tiled=True)  48.7 us
    ppermute x4, starting transfers between devices, butterfly_sum(): value = value + lax.ppermute(value, axis, pairs)  22 us
    mul x2, local copies, waits for them, and re-layouts, shards(): gathered.reshape(rows, points_here).astype(jnp.float32) * (1.0 / LINK_SCALE)  12.1 us
    all_to_all x1, starting transfers between devices, shards(): lax.all_to_all(sent, 'tm', split_axis=0, concat_axis=0, tiled=True)  10.8 us
    mul x2, other arithmetic, shards(): stacked * weights[None, :]  9.45 us
    reshape x1, local copies, waits for them, and re-layouts, shards(): square.reshape(tm_count, 2, local_blocks, tm_count, 2, local_blocks)  7.8 us
    mul x1, local copies, waits for them, and re-layouts, shards(): stacked * weights[None, :]  6.07 us
    dot_general x1, matrix products, shards(): jnp.dot(coeff, stacked, precision=THREE_PASS)  5.59 us
  transfers between devices with their start and end apart: 5, of which 4 were waited for; matrix products, arithmetic and copies ran while one was open for 5% of the time, Pallas kernels for 0%

profile of v2, /device:TPU:1, one launch (start us, length us, event | category | flops | bytes accessed | tf_op | source)
XLA Modules:
  0.0 156.8 jit_solution(3541051914515061602)
XLA Ops:
  0.6 0.0 copy-start
  0.7 0.7 multiply_reduce_fusion.1
  2.0 0.8 divide_convert_fusion.1
  2.9 0.0 copy-done
  2.9 0.7 fusion.3
  3.6 0.0 copy-start.1
  3.6 4.2 %copy.13 = f16[32,2,2,8192]{3,2,1,0:T(2,128)(2,1)} copy(f16[32,2,2,8192]{3,0,2,1:T(8,128)(2,1)S(1)} %fusion.3) | data formatting | bytes 4194304 | tf_op jit(solution)/shard_map/convert_element_type | solution.py:69
  7.8 10.8 %all-to-all-start = ((f16[32,2,2,8192]{3,2,1,0:T(2,128)(2,1)}), f16[32,2,2,8192]{3,2,1,0:T(2,128)(2,1)}, u32[]{:S(2)}, u32[]{:S(2)}) async-start(f16[32,2,2,8192]{3,2,1,0:T(2,128)(2,1)} %copy.13), calls=%async_computation | async-start | bytes 4194304 | tf_op jit(solution)/shard_map/all_to_all | solution.py:70
  18.6 0.0 copy-done.1
  18.6 48.7 %all-to-all-done = f16[32,2,2,8192]{3,2,1,0:T(2,128)(2,1)} async-done(((f16[32,2,2,8192]{3,2,1,0:T(2,128)(2,1)}), f16[32,2,2,8192]{3,2,1,0:T(2,128)(2,1)}, u32[]{:S(2)}, u32[]{:S(2)}) %all-to-all-start) | async-done | bytes 2097184 | tf_op jit(solution)/shard_map/all_to_all | solution.py:70
  67.3 9.4 %convert_multiply_fusion.1 = (f32[32,2,2,8192]{3,2,1,0:T(2,128)}, f32[32,2,2,8192]{3,2,1,0:T(2,128)}) fusion(f16[32,2,2,8192]{3,2,1,0:T(2,128)(2,1)} %all-to-all-done, f32[8192]{0:T(1024)S(1)} %broadcast_multiply_fusion), kind=kLoop, calls=%fused_computation.7 | loop fusion | flops 3145728 | bytes 10518528 | tf_op jit(solution)/shard_map/mul | solution.py:73
  76.7 6.0 %mul.130 = f32[128,8192]{1,0:T(8,128)} reshape(f32[32,2,2,8192]{3,2,1,0:T(2,128)} %get-tuple-element.3) | data formatting | bytes 8388608 | tf_op jit(solution)/shard_map/mul | solution.py:71
  82.8 6.1 %mul.127 = f32[128,8192]{1,0:T(8,128)} reshape(f32[32,2,2,8192]{3,2,1,0:T(2,128)} %get-tuple-element.2) | data formatting | bytes 8388608 | tf_op jit(solution)/shard_map/mul | solution.py:73
  88.8 5.4 %convolution_multiply_fusion.5 = f32[128,128]{1,0:T(8,128)S(1)} fusion(f32[128,8192]{1,0:T(8,128)} %mul.127, f32[128,8192]{1,0:T(8,128)} %mul.130), kind=kOutput, calls=%fused_computation.16 | convolution fusion | flops 805322752 | bytes 8454144 | tf_op jit(solution)/shard_map/dot_general | solution.py:73
  94.2 7.8 %reshape.68 = f32[32,2,2,32,2,2]{5,4,3,2,1,0:T(2,128)} reshape(f32[128,128]{1,0:T(8,128)S(1)} %convolution_multiply_fusion.5) | data formatting | bytes 131072 | tf_op jit(solution)/shard_map/reshape | solution.py:74
  102.0 4.7 %copy.14 = f32[2,32,2,2,32,2]{5,4,3,2,1,0:T(8,128)} copy(f32[2,32,2,2,32,2]{5,3,4,2,0,1:T(2,128)} %bitcast.64) | data formatting | bytes 131072 | tf_op jit(solution)/shard_map/transpose | solution.py:75
  106.8 4.0 %reshape.69 = f32[128,128]{1,0:T(8,128)S(1)} reshape(f32[2,32,2,2,32,2]{5,4,3,2,1,0:T(8,128)} %copy.14) | data formatting | bytes 131072 | tf_op jit(solution)/shard_map/reshape | solution.py:75
  110.8 0.1 fusion.11
  110.9 4.0 %collective-permute-start = (f32[2,64,64]{2,1,0:T(8,128)S(1)}, f32[2,64,64]{2,1,0:T(8,128)S(1)}, u32[]{:S(2)}, u32[]{:S(2)}) collective-permute-start(f32[2,64,64]{2,1,0:T(8,128)S(1)} %pad_maximum_fusion), channel_id=1, source_target_pairs={{0,1},{1,0},{2,3},{3,2},{4,5},{5,4},{6,7},{7,6},{8,9},{9,8},{10,11... | collective-permute-start | bytes 98312 | tf_op jit(solution)/shard_map/ppermute | solution.py:39
  114.9 0.9 collective-permute-done
  115.8 4.0 %collective-permute-start.1 = (f32[2,64,64]{2,1,0:T(8,128)S(1)}, f32[2,64,64]{2,1,0:T(8,128)S(1)}, u32[]{:S(2)}, u32[]{:S(2)}) collective-permute-start(f32[2,64,64]{2,1,0:T(8,128)S(1)} %fusion.22), channel_id=1, source_target_pairs={{0,2},{1,3},{2,0},{3,1},{4,6},{5,7},{6,4},{7,5},{8,10},{9,11},{10,... | collective-permute-start | bytes 98312 | tf_op jit(solution)/shard_map/ppermute | solution.py:39
  119.8 2.1 %collective-permute-done.1 = f32[2,64,64]{2,1,0:T(8,128)S(1)} collective-permute-done((f32[2,64,64]{2,1,0:T(8,128)S(1)}, f32[2,64,64]{2,1,0:T(8,128)S(1)}, u32[]{:S(2)}, u32[]{:S(2)}) %collective-permute-start.1) | collective-permute-done | bytes 32800 | tf_op jit(solution)/shard_map/ppermute | solution.py:39
  121.9 5.8 %collective-permute-start.2 = (f32[2,64,64]{2,1,0:T(8,128)S(1)}, f32[2,64,64]{2,1,0:T(8,128)S(1)}, u32[]{:S(2)}, u32[]{:S(2)}) collective-permute-start(f32[2,64,64]{2,1,0:T(8,128)S(1)} %fusion.51), channel_id=1, source_target_pairs={{0,4},{1,5},{2,6},{3,7},{4,0},{5,1},{6,2},{7,3},{8,12},{9,13},{10,... | collective-permute-start | bytes 98312 | tf_op jit(solution)/shard_map/ppermute | solution.py:39
  127.7 0.6 dynamic_slice.3
  128.3 1.0 collective-permute-done.2
  129.4 8.2 %collective-permute-start.3 = (f32[2,64,64]{2,1,0:T(8,128)S(1)}, f32[2,64,64]{2,1,0:T(8,128)S(1)}, u32[]{:S(2)}, u32[]{:S(2)}) collective-permute-start(f32[2,64,64]{2,1,0:T(8,128)S(1)} %add.32), channel_id=1, source_target_pairs={{0,8},{1,9},{2,10},{3,11},{4,12},{5,13},{6,14},{7,15},{8,0},{9,1},... | collective-permute-start | bytes 98312 | tf_op jit(solution)/shard_map/ppermute | solution.py:39
  137.6 0.7 iota_compare_fusion.4
  138.2 6.1 %reshape.74 = f32[128,8192,1]{1,0,2:T(8,128)} reshape(f32[32,2,2,8192]{3,2,1,0:T(2,128)} %get-tuple-element.3) | data formatting | bytes 8388608 | tf_op jit(solution)/shard_map/mul | solution.py:71
  144.3 0.0 collective-permute-done.3
  144.4 0.6 select_reduce_fusion
  145.0 0.7 multiply_reduce_fusion
  146.4 0.3 fusion.7
  146.6 0.3 fusion.12
  146.9 0.2 fusion.9
  147.1 0.2 fusion.6
  147.3 0.2 fusion.24
  147.5 0.2 fusion.23
  147.7 0.2 fusion.5
  147.9 0.2 fusion.26
  148.1 0.2 fusion.25
  148.3 0.2 fusion.4
  148.6 0.3 fusion.27
  148.9 0.1 slice_bitcast_fusion
  148.9 0.1 fusion.21
  149.0 0.1 maximum_maximum_fusion.1
  149.1 0.1 copy.15
  149.2 0.1 dot_general.57
  150.0 5.6 %fusion.2 = bf16[1,2,64,8192]{3,2,1,0:T(8,128)(2,1)} fusion(f32[128,8192,1]{1,0,2:T(8,128)} %reshape.74, pred[64]{0:T(512)(128)(4,1)S(1)} %iota_compare_fusion.4, f32[2,64,128]{1,0,2:T(2,128)S(1)} %dot_general.57), kind=kOutput, calls=%fused_computation.4 | convolution fusion | flops 807403520 | bytes 6357056 | tf_op jit(solution)/shard_map/dot_general | solution.py:93
  (12 shorter events, 0.1 us)
Async XLA Ops:
  0.6 2.2 %copy-start = (bf16[128,8192]{1,0:T(8,128)(2,1)S(1)}, bf16[128,8192]{1,0:T(8,128)(2,1)}, u32[]{:S(2)}) copy-start(bf16[128,8192]{1,0:T(8,128)(2,1)} %param.4) | copy-start | bytes 6291460
  3.6 15.0 %copy-start.1 = (f32[8192]{0:T(1024)S(1)}, f32[8192]{0:T(1024)}, u32[]{:S(2)}) copy-start(f32[8192]{0:T(1024)} %param.5) | copy-start | bytes 98308
  7.8 59.5 %all-to-all-start = ((f16[32,2,2,8192]{3,2,1,0:T(2,128)(2,1)}), f16[32,2,2,8192]{3,2,1,0:T(2,128)(2,1)}, u32[]{:S(2)}, u32[]{:S(2)}) async-start(f16[32,2,2,8192]{3,2,1,0:T(2,128)(2,1)} %copy.13), calls=%async_computation | async-start | bytes 4194304 | tf_op jit(solution)/shard_map/all_to_all | solution.py:70
  106.7 21.0 %copy-start.2 = (s32[32]{0:T(128)S(1)}, s32[32]{0:T(128)}, u32[]{:S(2)}) copy-start(s32[32]{0:T(128)} %param.7) | copy-start | bytes 388
  110.9 4.9 %collective-permute-start = (f32[2,64,64]{2,1,0:T(8,128)S(1)}, f32[2,64,64]{2,1,0:T(8,128)S(1)}, u32[]{:S(2)}, u32[]{:S(2)}) collective-permute-start(f32[2,64,64]{2,1,0:T(8,128)S(1)} %pad_maximum_fusion), channel_id=1, source_target_pairs={{0,1},{1,0},{2,3},{3,2},{4,5},{5,4},{6,7},{7,6},{8,9},{9,8},{10,11... | collective-permute-start | bytes 98312 | tf_op jit(solution)/shard_map/ppermute | solution.py:39
  115.8 6.1 %collective-permute-start.1 = (f32[2,64,64]{2,1,0:T(8,128)S(1)}, f32[2,64,64]{2,1,0:T(8,128)S(1)}, u32[]{:S(2)}, u32[]{:S(2)}) collective-permute-start(f32[2,64,64]{2,1,0:T(8,128)S(1)} %fusion.22), channel_id=1, source_target_pairs={{0,2},{1,3},{2,0},{3,1},{4,6},{5,7},{6,4},{7,5},{8,10},{9,11},{10,... | collective-permute-start | bytes 98312 | tf_op jit(solution)/shard_map/ppermute | solution.py:39
  121.9 7.5 %collective-permute-start.2 = (f32[2,64,64]{2,1,0:T(8,128)S(1)}, f32[2,64,64]{2,1,0:T(8,128)S(1)}, u32[]{:S(2)}, u32[]{:S(2)}) collective-permute-start(f32[2,64,64]{2,1,0:T(8,128)S(1)} %fusion.51), channel_id=1, source_target_pairs={{0,4},{1,5},{2,6},{3,7},{4,0},{5,1},{6,2},{7,3},{8,12},{9,13},{10,... | collective-permute-start | bytes 98312 | tf_op jit(solution)/shard_map/ppermute | solution.py:39
  129.4 15.0 %collective-permute-start.3 = (f32[2,64,64]{2,1,0:T(8,128)S(1)}, f32[2,64,64]{2,1,0:T(8,128)S(1)}, u32[]{:S(2)}, u32[]{:S(2)}) collective-permute-start(f32[2,64,64]{2,1,0:T(8,128)S(1)} %add.32), channel_id=1, source_target_pairs={{0,8},{1,9},{2,10},{3,11},{4,12},{5,13},{6,14},{7,15},{8,0},{9,1},... | collective-permute-start | bytes 98312 | tf_op jit(solution)/shard_map/ppermute | solution.py:39

commit v3 on v2

--- a/solution.py
+++ b/solution.py
@@ -2,11 +2,12 @@
 import jax.numpy as jnp
 from jax import lax
 from jax.sharding import PartitionSpec as P
+from jax.experimental import pallas as pl
+from jax.experimental.pallas import tpu as pltpu
 
 NT = 64
 NS_STEPS = 4
 HIGH = lax.Precision.HIGHEST
-THREE_PASS = lax.Precision.HIGH
 LINK_SCALE = 128.0
 
 
@@ -22,14 +23,93 @@
     return jnp.concatenate([real_rows, imag_rows], axis=0).astype(jnp.bfloat16)
 
 
-def transform_blocks(dft_table, snapshots, freq_count):
+def transform_blocks(dft_table, snapshots, freq_count, halves):
     local_blocks = snapshots.shape[0] // NT
-    point_count = snapshots.shape[1]
-    block_view = snapshots.reshape(local_blocks, NT, point_count)
-    table_view = dft_table.reshape(2, freq_count, NT)
-    return jnp.einsum(
-        "rft,btp->frbp", table_view, block_view, preferred_element_type=jnp.float32
-    )
+    points = snapshots.shape[1]
+    table_view = dft_table.reshape(2, freq_count, NT).transpose(1, 0, 2)
+    chooser = jnp.eye(local_blocks, dtype=dft_table.dtype)
+    lifted = table_view[:, :, None, None, :] * chooser[None, None, :, :, None]
+    lifted = lifted.reshape(freq_count * 2 * local_blocks, local_blocks * NT)
+    split_view = snapshots.reshape(local_blocks * NT, halves, points // halves)
+    spectra = jnp.einsum("qc,chp->qhp", lifted, split_view, preferred_element_type=jnp.float32)
+    return spectra.reshape(freq_count * 2 * local_blocks * halves, points // halves)
+
+
+def split_pair(value):
+    rounded = lax.reduce_precision(value, exponent_bits=8, mantissa_bits=7)
+    return rounded.astype(jnp.bfloat16), (value - rounded).astype(jnp.bfloat16)
+
+
+NT_DIMS = (((1,), (1,)), ((), ()))
+
+
+def gram_kernel(hi_ref, lo_ref, w_ref, o_ref):
+    @pl.when(pl.program_id(0) == 0)
+    def _():
+        o_ref[...] = jnp.zeros_like(o_ref)
+
+    x_hi = hi_ref[...]
+    x_lo = lo_ref[...]
+    x = x_hi.astype(jnp.float32) + x_lo.astype(jnp.float32)
+    odd = lax.broadcasted_iota(jnp.int32, x.shape, 0) % 2 == 1
+    row_weights = jnp.where(odd, w_ref[1:2, :], w_ref[0:1, :])
+    y_hi, y_lo = split_pair(x * row_weights)
+    acc = lax.dot_general(x_hi, y_hi, NT_DIMS, preferred_element_type=jnp.float32)
+    acc += lax.dot_general(x_lo, y_hi, NT_DIMS, preferred_element_type=jnp.float32)
+    acc += lax.dot_general(x_hi, y_lo, NT_DIMS, preferred_element_type=jnp.float32)
+    o_ref[...] += acc
+
+
+def gram_call(high, low, weights, chunk):
+    rows, points = high.shape
+    return pl.pallas_call(
+        gram_kernel,
+        grid=(points // chunk,),
+        in_specs=[
+            pl.BlockSpec((rows, chunk), lambda k: (0, k)),
+            pl.BlockSpec((rows, chunk), lambda k: (0, k)),
+            pl.BlockSpec((2, chunk), lambda k: (0, k)),
+        ],
+        out_specs=pl.BlockSpec((rows, rows), lambda k: (0, 0)),
+        out_shape=jax.ShapeDtypeStruct((rows, rows), jnp.float32),
+        cost_estimate=pl.CostEstimate(
+            flops=6 * rows * rows * points, transcendentals=0, bytes_accessed=4 * rows * points
+        ),
+    )(high, low, weights.reshape(2, points))
+
+
+def mode_kernel(c_hi_ref, c_lo_ref, hi_ref, lo_ref, o_ref):
+    x_hi = hi_ref[...]
+    x_lo = lo_ref[...]
+    c_hi = c_hi_ref[...]
+    acc = jnp.dot(c_hi, x_hi, preferred_element_type=jnp.float32)
+    acc += jnp.dot(c_lo_ref[...], x_hi, preferred_element_type=jnp.float32)
+    acc += jnp.dot(c_hi, x_lo, preferred_element_type=jnp.float32)
+    o_ref[...] = acc.astype(o_ref.dtype)
+
+
+def mode_call(coeff_halves, high, low, chunk):
+    halves, out_rows, rows = coeff_halves.shape
+    points = high.shape[1]
+    steps = points // chunk
+    c_hi, c_lo = split_pair(coeff_halves)
+    return pl.pallas_call(
+        mode_kernel,
+        grid=(halves, steps),
+        in_specs=[
+            pl.BlockSpec((None, out_rows, rows), lambda h, k: (h, 0, 0)),
+            pl.BlockSpec((None, out_rows, rows), lambda h, k: (h, 0, 0)),
+            pl.BlockSpec((rows, chunk), lambda h, k: (0, k)),
+            pl.BlockSpec((rows, chunk), lambda h, k: (0, k)),
+        ],
+        out_specs=pl.BlockSpec((out_rows, chunk), lambda h, k: (0, h * steps + k)),
+        out_shape=jax.ShapeDtypeStruct((out_rows, halves * points), jnp.bfloat16),
+        cost_estimate=pl.CostEstimate(
+            flops=6 * out_rows * rows * points * halves,
+            transcendentals=0,
+            bytes_accessed=4 * rows * points * halves + 2 * out_rows * points * halves,
+        ),
+    )(c_hi, c_lo, high, low)
 
 
 def butterfly_sum(value, axis, size):
@@ -65,14 +145,23 @@
     rows = 2 * block_count
 
     dft_table = spectra_table(freqs)
-    spectra = transform_blocks(dft_table, data, freq_count)
+    halves = 2
+    spectra = transform_blocks(dft_table, data, freq_count, halves)
     sent = (spectra * LINK_SCALE).astype(jnp.float16)
-    gathered = lax.all_to_all(sent, "tm", split_axis=0, concat_axis=0, tiled=True)
-    stacked = gathered.reshape(rows, points_here).astype(jnp.float32) * (1.0 / LINK_SCALE)
+    received = lax.all_to_all(sent, "tm", split_axis=0, concat_axis=0, tiled=True)
+    high, low = split_pair(received.astype(jnp.float32))
+    recv_rows = received.shape[0]
 
-    square = jnp.dot(stacked * weights[None, :], stacked.T, precision=THREE_PASS) / total_points
-    square = square.reshape(tm_count, 2, local_blocks, tm_count, 2, local_blocks)
-    square = square.transpose(1, 0, 2, 4, 3, 5).reshape(rows, rows)
+    square = gram_call(high, low, weights, 1024) * (1.0 / (LINK_SCALE * LINK_SCALE * total_points))
+    natural = jnp.arange(rows, dtype=jnp.int32)
+    part, block = natural // block_count, natural % block_count
+    home = (block // local_blocks) * (2 * local_blocks * halves) + part * (local_blocks * halves) + (block % local_blocks) * halves
+    recv_index = jnp.arange(recv_rows, dtype=jnp.int32)
+    pick = [(recv_index[None, :] == (home + h)[:, None]).astype(jnp.float32) for h in range(halves)]
+    same_half = recv_index[:, None] % halves == recv_index[None, :] % halves
+    either = pick[0] + pick[1]
+    square = jnp.where(same_half, square, jnp.zeros_like(square))
+    square = jnp.dot(jnp.dot(either, square, precision=HIGH), either.T, precision=HIGH)
     g_one = square[:block_count, :block_count] + square[block_count:, block_count:]
     g_two = square[:block_count, block_count:] - square[block_count:, :block_count]
     summed = butterfly_sum(jnp.stack([g_one, g_two]), "space", space_count)
@@ -89,12 +178,11 @@
         [jnp.concatenate([z_top.T, -z_low.T], axis=1), jnp.concatenate([z_low.T, z_top.T], axis=1)],
         axis=0,
     )
-    coeff = coeff.reshape(rows, 2, tm_count, local_blocks).transpose(0, 2, 1, 3).reshape(rows, rows)
-    modes = jnp.dot(coeff, stacked, precision=THREE_PASS).reshape(1, 2, block_count, points_here)
-
     kept_count = lax.dynamic_slice_in_dim(n_keep, lax.axis_index("tm"), 1)
-    kept_mask = jnp.arange(block_count, dtype=jnp.int32)[None, None, :, None] < kept_count[:, None, None, None]
-    mode_field = jnp.where(kept_mask, modes, jnp.zeros_like(modes)).astype(jnp.bfloat16)
+    kept_rows = jnp.arange(rows, dtype=jnp.int32) % block_count < kept_count
+    coeff = jnp.where(kept_rows[:, None], coeff, jnp.zeros_like(coeff)) * (1.0 / LINK_SCALE)
+    coeff_halves = jnp.stack([jnp.dot(coeff, p, precision=HIGH) for p in pick])
+    mode_field = mode_call(coeff_halves, high, low, 1024).reshape(1, 2, block_count, points_here)
     energy = (jnp.trace(g_one) / block_count).reshape(1)
     return (mode_field, energy)
 

time: 159 us -> 128 us (0.81)
  the two profiles are of different devices: /device:TPU:1 before, /device:TPU:16 now
where the time goes in v3:
time: 128 us; the launch traced here: 127 us
  waiting for transfers between devices  56.7 us (44%)
  starting transfers between devices  31.3 us (24%)
  Pallas kernels  14.4 us (11%)
  other arithmetic  7.33 us (6%)
  matrix products  6.95 us (5%)
  local copies, waits for them, and re-layouts  6.63 us (5%)
  between operations  4.06 us (3%)
    all_to_all x1, waiting for transfers between devices, shards(): lax.all_to_all(sent, 'tm', split_axis=0, concat_axis=0, tiled=True)  49.4 us
    ppermute x4, starting transfers between devices, butterfly_sum(): value = value + lax.ppermute(value, axis, pairs)  21.1 us
    all_to_all x1, starting transfers between devices, shards(): lax.all_to_all(sent, 'tm', split_axis=0, concat_axis=0, tiled=True)  10.2 us
    pallas_call x1, Pallas kernels, mode_call(): pl.pallas_call(mode_kernel, grid=(halves, steps), in_specs=[pl.BlockSpec(...  8.27 us
    ppermute x4, waiting for transfers between devices, butterfly_sum(): value = value + lax.ppermute(value, axis, pairs)  7.34 us
    pallas_call x1, Pallas kernels, gram_call(): pl.pallas_call(gram_kernel, grid=(points // chunk,), in_specs=[pl.BlockSp...  6.11 us
    convert_element_type x2, local copies, waits for them, and re-layouts, shards(): sent = (spectra * LINK_SCALE).astype(jnp.float16)  5.22 us
    convert_element_type x2, other arithmetic, split_pair(): (value - rounded).astype(jnp.bfloat16)  3.51 us
  transfers between devices with their start and end apart: 5, of which 5 were waited for; matrix products, arithmetic and copies ran while one was open for 1% of the time, Pallas kernels for 0%

profile of v3, /device:TPU:16, one launch (start us, length us, event | category | flops | bytes accessed | tf_op | source)
XLA Modules:
  0.0 127.4 jit_solution(5083140963775524034)
XLA Ops:
  0.6 0.6 multiply_reduce_fusion.1
  2.0 0.8 divide_convert_fusion.1
  2.9 0.1 broadcast_multiply_fusion
  3.0 0.1 reshape.159
  3.1 2.3 %fusion = f16[128,2,4096]{2,0,1:T(8,128)(2,1)S(1)} fusion(bf16[128,128,1]{1,0,2:T(8,128)(2,1)S(1)} %reshape.159, bf16[16,2,8,4096]{3,2,1,0:T(8,128)(2,1)} %bitcast.57), kind=kOutput, calls=%fused_computation.3 | convolution fusion | flops 270532608 | bytes 4227072 | tf_op jit(solution)/shard_map/qc,chp->qhp/dot_general | solution.py:34
  5.4 2.8 %copy.9 = f16[128,2,4096]{2,1,0:T(2,128)(2,1)S(1)} copy(f16[128,2,4096]{2,0,1:T(8,128)(2,1)S(1)} %fusion) | data formatting | bytes 4194304 | tf_op jit(solution)/shard_map/convert_element_type | solution.py:150
  8.3 2.4 %convert_element_type.72 = f16[32,8,4096]{2,1,0:T(8,128)(2,1)} reshape(f16[128,2,4096]{2,1,0:T(2,128)(2,1)S(1)} %copy.9) | data formatting | bytes 4194304 | tf_op jit(solution)/shard_map/convert_element_type | solution.py:150
  10.6 0.0 copy-start
  10.6 10.2 %all-to-all-start = ((f16[32,8,4096]{2,1,0:T(8,128)(2,1)}), f16[32,8,4096]{2,1,0:T(8,128)(2,1)S(1)}, u32[]{:S(2)}, u32[]{:S(2)}) async-start(f16[32,8,4096]{2,1,0:T(8,128)(2,1)} %convert_element_type.72), calls=%async_computation | async-start | bytes 4194304 | tf_op jit(solution)/shard_map/all_to_all | solution.py:151
  20.8 0.0 copy-done
  20.8 0.6 reshape.155.w_ref
  21.5 49.4 %all-to-all-done = f16[32,8,4096]{2,1,0:T(8,128)(2,1)S(1)} async-done(((f16[32,8,4096]{2,1,0:T(8,128)(2,1)}), f16[32,8,4096]{2,1,0:T(8,128)(2,1)S(1)}, u32[]{:S(2)}, u32[]{:S(2)}) %all-to-all-start) | async-done | bytes 2097184 | tf_op jit(solution)/shard_map/all_to_all | solution.py:151
  70.9 2.8 %fusion.1 = (bf16[256,4096]{1,0:T(8,128)(2,1)}, bf16[256,4096]{1,0:T(8,128)(2,1)}) fusion(f16[32,8,4096]{2,1,0:T(8,128)(2,1)S(1)} %all-to-all-done), kind=kLoop, calls=%fused_computation.4 | loop fusion | flops 5242880 | bytes 6291456 | tf_op jit(solution)/shard_map/convert_element_type | solution.py:40
  73.6 0.0 copy-start.1
  73.6 6.1 %shard_map.59 = f32[256,256]{1,0:T(8,128)} custom-call(bf16[256,4096]{1,0:T(8,128)(2,1)} %get-tuple-element.3.hi_ref, bf16[256,4096]{1,0:T(8,128)(2,1)} %get-tuple-element.2.lo_ref, f32[2,4096]{1,0:T(2,128)} %reshape.155.w_ref), custom_call_target="tpu_custom_call" | custom-call | flops 1610612736 | bytes 4194304 | tf_op jit(solution)/shard_map/pallas_call | solution.py:65
  79.7 1.3 %fusion.9 = f32[128,256]{1,0:T(8,128)S(1)} fusion(f32[256,256]{1,0:T(8,128)} %shard_map.59, s32[256]{0:T(256)S(1)} %and_select_fusion, s32[128]{0:T(128)S(1)} %get-tuple-element.19, s32[128]{0:T(128)S(1)} %get-tuple-element.18), kind=kOutput, calls=%fused_computation.21 | convolution fusion | flops 101023744 | bytes 395264 | tf_op jit(solution)/shard_map/dot_general | solution.py:164
  81.1 0.4 fusion.16
  81.5 0.1 fusion.32
  81.6 1.9 %collective-permute-start = (f32[2,64,64]{2,1,0:T(8,128)S(1)}, f32[2,64,64]{2,1,0:T(8,128)S(1)}, u32[]{:S(2)}, u32[]{:S(2)}) collective-permute-start(f32[2,64,64]{2,1,0:T(8,128)S(1)} %pad_maximum_fusion.1), channel_id=1, source_target_pairs={{0,1},{1,0},{2,3},{3,2},{4,5},{5,4},{6,7},{7,6},{8,9},{9,8},{10,11... | collective-permute-start | bytes 98312 | tf_op jit(solution)/shard_map/ppermute | solution.py:119
  83.5 1.2 collective-permute-done
  84.7 4.3 %collective-permute-start.1 = (f32[2,64,64]{2,1,0:T(8,128)S(1)}, f32[2,64,64]{2,1,0:T(8,128)S(1)}, u32[]{:S(2)}, u32[]{:S(2)}) collective-permute-start(f32[2,64,64]{2,1,0:T(8,128)S(1)} %fusion.51), channel_id=1, source_target_pairs={{0,2},{1,3},{2,0},{3,1},{4,6},{5,7},{6,4},{7,5},{8,10},{9,11},{10,... | collective-permute-start | bytes 98312 | tf_op jit(solution)/shard_map/ppermute | solution.py:119
  89.0 2.4 %collective-permute-done.1 = f32[2,64,64]{2,1,0:T(8,128)S(1)} collective-permute-done((f32[2,64,64]{2,1,0:T(8,128)S(1)}, f32[2,64,64]{2,1,0:T(8,128)S(1)}, u32[]{:S(2)}, u32[]{:S(2)}) %collective-permute-start.1) | collective-permute-done | bytes 32800 | tf_op jit(solution)/shard_map/ppermute | solution.py:119
  91.4 6.1 %collective-permute-start.2 = (f32[2,64,64]{2,1,0:T(8,128)S(1)}, f32[2,64,64]{2,1,0:T(8,128)S(1)}, u32[]{:S(2)}, u32[]{:S(2)}) collective-permute-start(f32[2,64,64]{2,1,0:T(8,128)S(1)} %fusion.77), channel_id=1, source_target_pairs={{0,4},{1,5},{2,6},{3,7},{4,0},{5,1},{6,2},{7,3},{8,12},{9,13},{10,... | collective-permute-start | bytes 98312 | tf_op jit(solution)/shard_map/ppermute | solution.py:119
  97.5 0.0 copy-done.1
  97.5 0.6 dynamic_slice.3
  98.1 1.9 %collective-permute-done.2 = f32[2,64,64]{2,1,0:T(8,128)S(1)} collective-permute-done((f32[2,64,64]{2,1,0:T(8,128)S(1)}, f32[2,64,64]{2,1,0:T(8,128)S(1)}, u32[]{:S(2)}, u32[]{:S(2)}) %collective-permute-start.2) | collective-permute-done | bytes 32800 | tf_op jit(solution)/shard_map/ppermute | solution.py:119
  100.1 8.8 %collective-permute-start.3 = (f32[2,64,64]{2,1,0:T(8,128)S(1)}, f32[2,64,64]{2,1,0:T(8,128)S(1)}, u32[]{:S(2)}, u32[]{:S(2)}) collective-permute-start(f32[2,64,64]{2,1,0:T(8,128)S(1)} %add.167), channel_id=1, source_target_pairs={{0,8},{1,9},{2,10},{3,11},{4,12},{5,13},{6,14},{7,15},{8,0},{9,1},... | collective-permute-start | bytes 98312 | tf_op jit(solution)/shard_map/ppermute | solution.py:119
  108.9 0.7 broadcast_compare_fusion
  109.6 1.8 %collective-permute-done.3 = f32[2,64,64]{2,1,0:T(8,128)S(1)} collective-permute-done((f32[2,64,64]{2,1,0:T(8,128)S(1)}, f32[2,64,64]{2,1,0:T(8,128)S(1)}, u32[]{:S(2)}, u32[]{:S(2)}) %collective-permute-start.3) | collective-permute-done | bytes 32800 | tf_op jit(solution)/shard_map/ppermute | solution.py:119
  111.4 0.6 select_reduce_fusion
  112.0 0.7 multiply_reduce_fusion
  113.4 0.3 fusion.7
  113.6 0.3 fusion.33
  113.9 0.2 fusion.30
  114.1 0.2 fusion.6
  114.3 0.2 fusion.53
  114.5 0.2 fusion.52
  114.7 0.2 fusion.5
  114.9 0.2 fusion.54
  115.1 0.2 fusion.55
  115.4 0.2 fusion.4
  115.6 0.3 fusion.56
  115.9 0.1 fusion.50
  115.9 0.1 slice_bitcast_fusion
  116.0 0.3 convolution_bitcast_fusion.1
  116.3 0.3 convolution_bitcast_fusion
  117.2 0.7 fusion.8
  118.0 8.3 %shard_map.60 = bf16[128,8192]{1,0:T(8,128)(2,1)} custom-call(bf16[2,128,256]{2,1,0:T(8,128)(2,1)} %get-tuple-element.5.c_hi_ref, bf16[2,128,256]{2,1,0:T(8,128)(2,1)} %get-tuple-element.4.c_lo_ref, bf16[256,4096]{1,0:T(8,128)(2,1)} %get-tuple-element.3.hi_ref, bf16[256,4096]{1,0:T(8,128)(2,1)} %get-tuple-element.2.lo_ref), custom_call_target="tpu_custom_call" | custom-call | flops 1610612736 | bytes 10485760 | tf_op jit(solution)/shard_map/pallas_call | solution.py:96
  (12 shorter events, 0.1 us)
Async XLA Ops:
  10.6 10.2 %copy-start = (f32[8192]{0:T(1024)S(1)}, f32[8192]{0:T(1024)}, u32[]{:S(2)}) copy-start(f32[8192]{0:T(1024)} %param.5) | copy-start | bytes 98308
  10.6 60.2 %all-to-all-start = ((f16[32,8,4096]{2,1,0:T(8,128)(2,1)}), f16[32,8,4096]{2,1,0:T(8,128)(2,1)S(1)}, u32[]{:S(2)}, u32[]{:S(2)}) async-start(f16[32,8,4096]{2,1,0:T(8,128)(2,1)} %convert_element_type.72), calls=%async_computation | async-start | bytes 4194304 | tf_op jit(solution)/shard_map/all_to_all | solution.py:151
  73.6 23.9 %copy-start.1 = (s32[32]{0:T(128)S(1)}, s32[32]{0:T(128)}, u32[]{:S(2)}) copy-start(s32[32]{0:T(128)} %param.7) | copy-start | bytes 388
  81.6 3.1 %collective-permute-start = (f32[2,64,64]{2,1,0:T(8,128)S(1)}, f32[2,64,64]{2,1,0:T(8,128)S(1)}, u32[]{:S(2)}, u32[]{:S(2)}) collective-permute-start(f32[2,64,64]{2,1,0:T(8,128)S(1)} %pad_maximum_fusion.1), channel_id=1, source_target_pairs={{0,1},{1,0},{2,3},{3,2},{4,5},{5,4},{6,7},{7,6},{8,9},{9,8},{10,11... | collective-permute-start | bytes 98312 | tf_op jit(solution)/shard_map/ppermute | solution.py:119
  84.7 6.7 %collective-permute-start.1 = (f32[2,64,64]{2,1,0:T(8,128)S(1)}, f32[2,64,64]{2,1,0:T(8,128)S(1)}, u32[]{:S(2)}, u32[]{:S(2)}) collective-permute-start(f32[2,64,64]{2,1,0:T(8,128)S(1)} %fusion.51), channel_id=1, source_target_pairs={{0,2},{1,3},{2,0},{3,1},{4,6},{5,7},{6,4},{7,5},{8,10},{9,11},{10,... | collective-permute-start | bytes 98312 | tf_op jit(solution)/shard_map/ppermute | solution.py:119
  91.4 8.6 %collective-permute-start.2 = (f32[2,64,64]{2,1,0:T(8,128)S(1)}, f32[2,64,64]{2,1,0:T(8,128)S(1)}, u32[]{:S(2)}, u32[]{:S(2)}) collective-permute-start(f32[2,64,64]{2,1,0:T(8,128)S(1)} %fusion.77), channel_id=1, source_target_pairs={{0,4},{1,5},{2,6},{3,7},{4,0},{5,1},{6,2},{7,3},{8,12},{9,13},{10,... | collective-permute-start | bytes 98312 | tf_op jit(solution)/shard_map/ppermute | solution.py:119
  100.1 11.3 %collective-permute-start.3 = (f32[2,64,64]{2,1,0:T(8,128)S(1)}, f32[2,64,64]{2,1,0:T(8,128)S(1)}, u32[]{:S(2)}, u32[]{:S(2)}) collective-permute-start(f32[2,64,64]{2,1,0:T(8,128)S(1)} %add.167), channel_id=1, source_target_pairs={{0,8},{1,9},{2,10},{3,11},{4,12},{5,13},{6,14},{7,15},{8,0},{9,1},... | collective-permute-start | bytes 98312 | tf_op jit(solution)/shard_map/ppermute | solution.py:119

commit v4 on v3

--- a/solution.py
+++ b/solution.py
@@ -164,9 +164,15 @@
     square = jnp.dot(jnp.dot(either, square, precision=HIGH), either.T, precision=HIGH)
     g_one = square[:block_count, :block_count] + square[block_count:, block_count:]
     g_two = square[:block_count, block_count:] - square[block_count:, :block_count]
-    summed = butterfly_sum(jnp.stack([g_one, g_two]), "space", space_count)
-    g_one = summed[0]
-    g_two = summed[1]
+    lower = jnp.arange(block_count)[:, None] > jnp.arange(block_count)[None, :]
+    packed = jnp.where(lower, g_two, g_one)
+    spread = jnp.broadcast_to(packed[None], (space_count, block_count, block_count))
+    partials = lax.all_to_all(spread, "space", split_axis=0, concat_axis=0, tiled=True)
+    total = jnp.sum(partials, axis=0)
+    upper = jnp.where(lower, jnp.zeros_like(total), total)
+    strict = jnp.where(lower, total, jnp.zeros_like(total))
+    g_one = upper + jnp.where(lower, upper.T, jnp.zeros_like(total))
+    g_two = strict - strict.T
 
     embedded = jnp.concatenate(
         [jnp.concatenate([g_one, -g_two], axis=1), jnp.concatenate([g_two, g_one], axis=1)], axis=0

time: 128 us -> 125 us (0.977)
  the two profiles are of different devices: /device:TPU:16 before, /device:TPU:1 now
where the time goes in v4:
time: 125 us; the launch traced here: 124 us
  waiting for transfers between devices  58.6 us (47%)
  starting transfers between devices  23.1 us (18%)
  Pallas kernels  14.4 us (12%)
  other arithmetic  8.59 us (7%)
  local copies, waits for them, and re-layouts  8.49 us (7%)
  matrix products  6.97 us (6%)
  between operations  4.03 us (3%)
    all_to_all x1, waiting for transfers between devices, shards(): lax.all_to_all(sent, 'tm', split_axis=0, concat_axis=0, tiled=True)  48.3 us
    all_to_all x1, starting transfers between devices, shards(): lax.all_to_all(spread, 'space', split_axis=0, concat_axis=0, tiled=True)  12.5 us
    all_to_all x1, starting transfers between devices, shards(): lax.all_to_all(sent, 'tm', split_axis=0, concat_axis=0, tiled=True)  10.6 us
    all_to_all x1, waiting for transfers between devices, shards(): lax.all_to_all(spread, 'space', split_axis=0, concat_axis=0, tiled=True)  10.3 us
    pallas_call x1, Pallas kernels, mode_call(): pl.pallas_call(mode_kernel, grid=(halves, steps), in_specs=[pl.BlockSpec(...  8.27 us
    pallas_call x1, Pallas kernels, gram_call(): pl.pallas_call(gram_kernel, grid=(points // chunk,), in_specs=[pl.BlockSp...  6.1 us
    convert_element_type x2, local copies, waits for them, and re-layouts, shards(): sent = (spectra * LINK_SCALE).astype(jnp.float16)  5.22 us
    convert_element_type x2, other arithmetic, split_pair(): (value - rounded).astype(jnp.bfloat16)  3.51 us
  transfers between devices with their start and end apart: 2, of which 2 were waited for; matrix products, arithmetic and copies ran while one was open for 2% of the time, Pallas kernels for 0%

profile of v4, /device:TPU:1, one launch (start us, length us, event | category | flops | bytes accessed | tf_op | source)
XLA Modules:
  0.0 124.2 jit_solution(384972966028618028)
XLA Ops:
  0.6 0.6 multiply_reduce_fusion.1
  2.0 0.8 divide_convert_fusion.1
  2.9 0.1 broadcast_multiply_fusion
  3.0 0.1 reshape.160
  3.1 2.3 %fusion = f16[128,2,4096]{2,0,1:T(8,128)(2,1)S(1)} fusion(bf16[128,128,1]{1,0,2:T(8,128)(2,1)S(1)} %reshape.160, bf16[16,2,8,4096]{3,2,1,0:T(8,128)(2,1)} %bitcast.56), kind=kOutput, calls=%fused_computation.3 | convolution fusion | flops 270532608 | bytes 4227072 | tf_op jit(solution)/shard_map/qc,chp->qhp/dot_general | solution.py:34
  5.4 2.8 %copy.20 = f16[128,2,4096]{2,1,0:T(2,128)(2,1)S(1)} copy(f16[128,2,4096]{2,0,1:T(8,128)(2,1)S(1)} %fusion) | data formatting | bytes 4194304 | tf_op jit(solution)/shard_map/convert_element_type | solution.py:150
  8.3 2.4 %convert_element_type.72 = f16[32,8,4096]{2,1,0:T(8,128)(2,1)} reshape(f16[128,2,4096]{2,1,0:T(2,128)(2,1)S(1)} %copy.20) | data formatting | bytes 4194304 | tf_op jit(solution)/shard_map/convert_element_type | solution.py:150
  10.6 0.0 copy-start
  10.6 10.6 %all-to-all-start = ((f16[32,8,4096]{2,1,0:T(8,128)(2,1)}), f16[32,8,4096]{2,1,0:T(8,128)(2,1)S(1)}, u32[]{:S(2)}, u32[]{:S(2)}) async-start(f16[32,8,4096]{2,1,0:T(8,128)(2,1)} %convert_element_type.72), calls=%async_computation | async-start | bytes 4194304 | tf_op jit(solution)/shard_map/all_to_all | solution.py:151
  21.3 0.0 copy-done
  21.3 0.6 reshape.156.w_ref
  21.9 48.3 %all-to-all-done = f16[32,8,4096]{2,1,0:T(8,128)(2,1)S(1)} async-done(((f16[32,8,4096]{2,1,0:T(8,128)(2,1)}), f16[32,8,4096]{2,1,0:T(8,128)(2,1)S(1)}, u32[]{:S(2)}, u32[]{:S(2)}) %all-to-all-start) | async-done | bytes 2097184 | tf_op jit(solution)/shard_map/all_to_all | solution.py:151
  70.2 2.8 %fusion.1 = (bf16[256,4096]{1,0:T(8,128)(2,1)}, bf16[256,4096]{1,0:T(8,128)(2,1)}) fusion(f16[32,8,4096]{2,1,0:T(8,128)(2,1)S(1)} %all-to-all-done), kind=kLoop, calls=%fused_computation.4 | loop fusion | flops 5242880 | bytes 6291456 | tf_op jit(solution)/shard_map/convert_element_type | solution.py:40
  72.9 6.1 %shard_map.59 = f32[256,256]{1,0:T(8,128)} custom-call(bf16[256,4096]{1,0:T(8,128)(2,1)} %get-tuple-element.7.hi_ref, bf16[256,4096]{1,0:T(8,128)(2,1)} %get-tuple-element.6.lo_ref, f32[2,4096]{1,0:T(2,128)} %reshape.156.w_ref), custom_call_target="tpu_custom_call" | custom-call | flops 1610612736 | bytes 4194304 | tf_op jit(solution)/shard_map/pallas_call | solution.py:65
  79.0 0.0 copy-start.1
  79.0 1.4 %fusion.9 = f32[128,256]{1,0:T(8,128)S(1)} fusion(f32[256,256]{1,0:T(8,128)} %shard_map.59, s32[256]{0:T(256)S(1)} %and_select_fusion, s32[128]{0:T(128)S(1)} %get-tuple-element.19, s32[128]{0:T(128)S(1)} %get-tuple-element.18), kind=kOutput, calls=%fused_computation.21 | convolution fusion | flops 101023744 | bytes 395264 | tf_op jit(solution)/shard_map/dot_general | solution.py:164
  80.4 0.4 fusion.16
  80.8 0.1 fusion.31
  80.9 1.0 reshape.162
  81.9 12.5 %all-to-all-start.1 = ((f32[16,1,4096]{2,1,0:T(1,128)}), f32[16,1,4096]{2,1,0:T(1,128)S(1)}, u32[]{:S(2)}, u32[]{:S(2)}) async-start(f32[16,1,4096]{2,1,0:T(1,128)} %reshape.162), calls=%async_computation.1 | async-start | bytes 524288 | tf_op jit(solution)/shard_map/all_to_all | solution.py:170
  94.5 0.0 copy-done.1
  94.5 0.6 dynamic_slice.3
  95.1 0.7 broadcast_compare_fusion
  95.7 10.3 %all-to-all-done.1 = f32[16,1,4096]{2,1,0:T(1,128)S(1)} async-done(((f32[16,1,4096]{2,1,0:T(1,128)}), f32[16,1,4096]{2,1,0:T(1,128)S(1)}, u32[]{:S(2)}, u32[]{:S(2)}) %all-to-all-start.1) | async-done | bytes 262176 | tf_op jit(solution)/shard_map/all_to_all | solution.py:170
  106.0 0.5 broadcast.370
  106.6 1.3 %reduce = f32[16,4096]{1,0:T(8,128)S(1)} reduce(f32[16,1,4096]{2,1,0:T(1,128)S(1)} %all-to-all-done.1, f32[]{:T(128)} %broadcast.370), dimensions={1}, to_apply=%all_to_all.8.reduce_sub_computation | reduce | bytes 524292 | tf_op jit(solution)/shard_map/all_to_all | solution.py:170
  107.8 0.2 reshape.163
  108.1 0.1 copy.21
  108.2 0.6 fusion.53
  108.8 0.7 multiply_reduce_fusion
  110.2 0.3 fusion.7
  110.5 0.3 fusion.35
  110.7 0.2 fusion.30
  110.9 0.2 fusion.6
  111.1 0.2 fusion.56
  111.3 0.2 fusion.55
  111.5 0.2 fusion.5
  111.8 0.2 fusion.57
  112.0 0.2 fusion.58
  112.2 0.2 fusion.4
  112.4 0.3 fusion.59
  112.7 0.1 fusion.51
  112.8 0.1 slice_bitcast_fusion
  112.8 0.3 convolution_bitcast_fusion.1
  113.1 0.3 convolution_bitcast_fusion
  114.1 0.7 fusion.8
  114.8 8.3 %shard_map.60 = bf16[128,8192]{1,0:T(8,128)(2,1)} custom-call(bf16[2,128,256]{2,1,0:T(8,128)(2,1)} %get-tuple-element.9.c_hi_ref, bf16[2,128,256]{2,1,0:T(8,128)(2,1)} %get-tuple-element.8.c_lo_ref, bf16[256,4096]{1,0:T(8,128)(2,1)} %get-tuple-element.7.hi_ref, bf16[256,4096]{1,0:T(8,128)(2,1)} %get-tuple-element.6.lo_ref), custom_call_target="tpu_custom_call" | custom-call | flops 1610612736 | bytes 10485760 | tf_op jit(solution)/shard_map/pallas_call | solution.py:96
  (8 shorter events, 0.2 us)
Async XLA Ops:
  10.6 10.6 %copy-start = (f32[8192]{0:T(1024)S(1)}, f32[8192]{0:T(1024)}, u32[]{:S(2)}) copy-start(f32[8192]{0:T(1024)} %param.5) | copy-start | bytes 98308
  10.6 59.5 %all-to-all-start = ((f16[32,8,4096]{2,1,0:T(8,128)(2,1)}), f16[32,8,4096]{2,1,0:T(8,128)(2,1)S(1)}, u32[]{:S(2)}, u32[]{:S(2)}) async-start(f16[32,8,4096]{2,1,0:T(8,128)(2,1)} %convert_element_type.72), calls=%async_computation | async-start | bytes 4194304 | tf_op jit(solution)/shard_map/all_to_all | solution.py:151
  79.0 15.4 %copy-start.1 = (s32[32]{0:T(128)S(1)}, s32[32]{0:T(128)}, u32[]{:S(2)}) copy-start(s32[32]{0:T(128)} %param.7) | copy-start | bytes 388
  81.9 24.1 %all-to-all-start.1 = ((f32[16,1,4096]{2,1,0:T(1,128)}), f32[16,1,4096]{2,1,0:T(1,128)S(1)}, u32[]{:S(2)}, u32[]{:S(2)}) async-start(f32[16,1,4096]{2,1,0:T(1,128)} %reshape.162), calls=%async_computation.1 | async-start | bytes 524288 | tf_op jit(solution)/shard_map/all_to_all | solution.py:170

commit v5 on v4

--- a/solution.py
+++ b/solution.py
@@ -1,3 +1,5 @@
+import functools
+
 import jax
 import jax.numpy as jnp
 from jax import lax
@@ -25,14 +27,18 @@
 
 def transform_blocks(dft_table, snapshots, freq_count, halves):
     local_blocks = snapshots.shape[0] // NT
-    points = snapshots.shape[1]
+    points = snapshots.shape[1] // halves
     table_view = dft_table.reshape(2, freq_count, NT).transpose(1, 0, 2)
     chooser = jnp.eye(local_blocks, dtype=dft_table.dtype)
-    lifted = table_view[:, :, None, None, :] * chooser[None, None, :, :, None]
-    lifted = lifted.reshape(freq_count * 2 * local_blocks, local_blocks * NT)
-    split_view = snapshots.reshape(local_blocks * NT, halves, points // halves)
-    spectra = jnp.einsum("qc,chp->qhp", lifted, split_view, preferred_element_type=jnp.float32)
-    return spectra.reshape(freq_count * 2 * local_blocks * halves, points // halves)
+    halver = jnp.eye(halves, dtype=dft_table.dtype)
+    lifted = (
+        table_view[:, None, :, None, None, None, :]
+        * halver[None, :, None, None, :, None, None]
+        * chooser[None, None, None, :, None, :, None]
+    )
+    lifted = lifted.reshape(freq_count * halves * 2 * local_blocks, halves * local_blocks * NT)
+    stacked = jnp.concatenate([snapshots[:, h * points:(h + 1) * points] for h in range(halves)], axis=0)
+    return jnp.dot(lifted, stacked, preferred_element_type=jnp.float32)
 
 
 def split_pair(value):
@@ -43,7 +49,7 @@
 NT_DIMS = (((1,), (1,)), ((), ()))
 
 
-def gram_kernel(hi_ref, lo_ref, w_ref, o_ref):
+def gram_kernel(group, hi_ref, lo_ref, w_ref, o_ref):
     @pl.when(pl.program_id(0) == 0)
     def _():
         o_ref[...] = jnp.zeros_like(o_ref)
@@ -51,7 +57,7 @@
     x_hi = hi_ref[...]
     x_lo = lo_ref[...]
     x = x_hi.astype(jnp.float32) + x_lo.astype(jnp.float32)
-    odd = lax.broadcasted_iota(jnp.int32, x.shape, 0) % 2 == 1
+    odd = lax.broadcasted_iota(jnp.int32, x.shape, 0) // group % 2 == 1
     row_weights = jnp.where(odd, w_ref[1:2, :], w_ref[0:1, :])
     y_hi, y_lo = split_pair(x * row_weights)
     acc = lax.dot_general(x_hi, y_hi, NT_DIMS, preferred_element_type=jnp.float32)
@@ -60,10 +66,10 @@
     o_ref[...] += acc
 
 
-def gram_call(high, low, weights, chunk):
+def gram_call(high, low, weights, chunk, group):
     rows, points = high.shape
     return pl.pallas_call(
-        gram_kernel,
+        functools.partial(gram_kernel, group),
         grid=(points // chunk,),
         in_specs=[
             pl.BlockSpec((rows, chunk), lambda k: (0, k)),
@@ -152,13 +158,15 @@
     high, low = split_pair(received.astype(jnp.float32))
     recv_rows = received.shape[0]
 
-    square = gram_call(high, low, weights, 1024) * (1.0 / (LINK_SCALE * LINK_SCALE * total_points))
+    square = gram_call(high, low, weights, 1024, 2 * local_blocks) * (1.0 / (LINK_SCALE * LINK_SCALE * total_points))
     natural = jnp.arange(rows, dtype=jnp.int32)
     part, block = natural // block_count, natural % block_count
-    home = (block // local_blocks) * (2 * local_blocks * halves) + part * (local_blocks * halves) + (block % local_blocks) * halves
+    group = 2 * local_blocks
+    home = (block // local_blocks) * (group * halves) + part * local_blocks + block % local_blocks
     recv_index = jnp.arange(recv_rows, dtype=jnp.int32)
-    pick = [(recv_index[None, :] == (home + h)[:, None]).astype(jnp.float32) for h in range(halves)]
-    same_half = recv_index[:, None] % halves == recv_index[None, :] % halves
+    pick = [(recv_index[None, :] == (home + h * group)[:, None]).astype(jnp.float32) for h in range(halves)]
+    row_half = recv_index // group % halves
+    same_half = row_half[:, None] == row_half[None, :]
     either = pick[0] + pick[1]
     square = jnp.where(same_half, square, jnp.zeros_like(square))
     square = jnp.dot(jnp.dot(either, square, precision=HIGH), either.T, precision=HIGH)
@@ -188,7 +196,7 @@
     kept_rows = jnp.arange(rows, dtype=jnp.int32) % block_count < kept_count
     coeff = jnp.where(kept_rows[:, None], coeff, jnp.zeros_like(coeff)) * (1.0 / LINK_SCALE)
     coeff_halves = jnp.stack([jnp.dot(coeff, p, precision=HIGH) for p in pick])
-    mode_field = mode_call(coeff_halves, high, low, 1024).reshape(1, 2, block_count, points_here)
+    mode_field = mode_call(coeff_halves, high, low, 2048).reshape(1, 2, block_count, points_here)
     energy = (jnp.trace(g_one) / block_count).reshape(1)
     return (mode_field, energy)
 

time: 125 us -> 119 us (0.952)
  local copies, waits for them, and re-layouts: 8.49 us -> 5.07 us
  Pallas kernels: 14.4 us -> 12.4 us
    convert_element_type x2 -> x0, local copies, waits for them, and re-layouts: 5.22 us -> none  [shards(): sent = (spectra * LINK_SCALE).astype(jnp.float16)]
    pallas_call x1, Pallas kernels: 8.27 us -> 6.3 us  [mode_call(): pl.pallas_call(mode_kernel, grid=(halves, steps), in_specs=[pl.BlockSpec(...]
    slice x0 -> x1, local copies, waits for them, and re-layouts: none -> 1.68 us  [transform_blocks(): snapshots[:, h * points:(h + 1) * points]]
where the time goes in v5:
time: 119 us
  waiting for transfers between devices  58.6 us (49%)
  starting transfers between devices  23.1 us (19%)
  Pallas kernels  12.4 us (10%)
  other arithmetic  8.87 us (7%)
  matrix products  6.73 us (6%)
  local copies, waits for them, and re-layouts  5.07 us (4%)
  between operations  4.02 us (3%)
    all_to_all x1, waiting for transfers between devices, shards(): lax.all_to_all(sent, 'tm', split_axis=0, concat_axis=0, tiled=True)  48.3 us
    all_to_all x1, starting transfers between devices, shards(): lax.all_to_all(spread, 'space', split_axis=0, concat_axis=0, tiled=True)  12.5 us
    all_to_all x1, starting transfers between devices, shards(): lax.all_to_all(sent, 'tm', split_axis=0, concat_axis=0, tiled=True)  10.6 us
    all_to_all x1, waiting for transfers between devices, shards(): lax.all_to_all(spread, 'space', split_axis=0, concat_axis=0, tiled=True)  10.3 us
    pallas_call x1, Pallas kernels, mode_call(): pl.pallas_call(mode_kernel, grid=(halves, steps), in_specs=[pl.BlockSpec(...  6.3 us
    pallas_call x1, Pallas kernels, gram_call(): pl.pallas_call(functools.partial(gram_kernel, group), grid=(points // chu...  6.13 us
    convert_element_type x2, other arithmetic, split_pair(): (value - rounded).astype(jnp.bfloat16)  3.51 us
  transfers between devices with their start and end apart: 2, of which 2 were waited for; matrix products, arithmetic and copies ran while one was open for 2% of the time, Pallas kernels for 0%

profile of v5, /device:TPU:1, one launch (start us, length us, event | category | flops | bytes accessed | tf_op | source)
XLA Modules:
  0.0 118.8 jit_solution(14993491602417790955)
XLA Ops:
  0.6 0.6 multiply_reduce_fusion.1
  2.0 0.8 divide_convert_fusion.1
  2.9 0.1 broadcast_multiply_fusion.1
  3.0 0.3 broadcast_multiply_fusion
  3.3 0.2 mul.187
  3.5 1.7 %fusion.58 = (bf16[128,4096]{1,0:T(8,128)(2,1)S(1)}, bf16[128,4096]{1,0:T(8,128)(2,1)S(1)}) fusion(bf16[128,8192]{1,0:T(8,128)(2,1)} %param.4), kind=kLoop, calls=%fused_computation.111 | loop fusion | bytes 4194304 | tf_op jit(solution)/shard_map/slice | solution.py:40
  5.2 2.1 %fusion.1 = f16[32,8,4096]{2,1,0:T(8,128)(2,1)} fusion(bf16[256,256]{1,0:T(8,128)(2,1)S(1)} %mul.187, bf16[128,4096]{1,0:T(8,128)(2,1)S(1)} %get-tuple-element.9, bf16[128,4096]{1,0:T(8,128)(2,1)S(1)} %get-tuple-element.8), kind=kOutput, calls=%fused_computation.4 | convolution fusion | flops 543162368 | bytes 4325376 | tf_op jit(solution)/shard_map/dot_general | solution.py:41
  7.2 0.0 copy-start
  7.2 10.6 %all-to-all-start = ((f16[32,8,4096]{2,1,0:T(8,128)(2,1)}), f16[32,8,4096]{2,1,0:T(8,128)(2,1)S(1)}, u32[]{:S(2)}, u32[]{:S(2)}) async-start(f16[32,8,4096]{2,1,0:T(8,128)(2,1)} %fusion.1), calls=%async_computation | async-start | bytes 4194304 | tf_op jit(solution)/shard_map/all_to_all | solution.py:157
  17.9 0.0 copy-done
  17.9 0.6 reshape.170.w_ref
  18.5 48.3 %all-to-all-done = f16[32,8,4096]{2,1,0:T(8,128)(2,1)S(1)} async-done(((f16[32,8,4096]{2,1,0:T(8,128)(2,1)}), f16[32,8,4096]{2,1,0:T(8,128)(2,1)S(1)}, u32[]{:S(2)}, u32[]{:S(2)}) %all-to-all-start) | async-done | bytes 2097184 | tf_op jit(solution)/shard_map/all_to_all | solution.py:157
  66.8 2.8 %fusion.2 = (bf16[256,4096]{1,0:T(8,128)(2,1)}, bf16[256,4096]{1,0:T(8,128)(2,1)}) fusion(f16[32,8,4096]{2,1,0:T(8,128)(2,1)S(1)} %all-to-all-done), kind=kLoop, calls=%fused_computation.5 | loop fusion | flops 5242880 | bytes 6291456 | tf_op jit(solution)/shard_map/convert_element_type | solution.py:46
  69.6 6.1 %shard_map.59 = f32[256,256]{1,0:T(8,128)} custom-call(bf16[256,4096]{1,0:T(8,128)(2,1)} %get-tuple-element.7.hi_ref, bf16[256,4096]{1,0:T(8,128)(2,1)} %get-tuple-element.6.lo_ref, f32[2,4096]{1,0:T(2,128)} %reshape.170.w_ref), custom_call_target="tpu_custom_call" | custom-call | flops 1610612736 | bytes 4194304 | tf_op jit(solution)/shard_map/pallas_call | solution.py:71
  75.7 0.0 copy-start.1
  75.7 1.3 %fusion.11 = f32[128,256]{1,0:T(8,128)S(1)} fusion(f32[256,256]{1,0:T(8,128)} %shard_map.59, s32[256]{0:T(256)S(1)} %and_select_fusion, s32[128]{0:T(128)S(1)} %get-tuple-element.21, s32[128]{0:T(128)S(1)} %get-tuple-element.20), kind=kOutput, calls=%fused_computation.23 | convolution fusion | flops 101023744 | bytes 395264 | tf_op jit(solution)/shard_map/dot_general | solution.py:172
  77.0 0.4 fusion.18
  77.4 0.1 fusion.33
  77.5 1.0 reshape.174
  78.6 12.5 %all-to-all-start.1 = ((f32[16,1,4096]{2,1,0:T(1,128)}), f32[16,1,4096]{2,1,0:T(1,128)S(1)}, u32[]{:S(2)}, u32[]{:S(2)}) async-start(f32[16,1,4096]{2,1,0:T(1,128)} %reshape.174), calls=%async_computation.1 | async-start | bytes 524288 | tf_op jit(solution)/shard_map/all_to_all | solution.py:178
  91.1 0.0 copy-done.1
  91.1 0.6 dynamic_slice.3
  91.7 0.7 broadcast_compare_fusion
  92.3 10.3 %all-to-all-done.1 = f32[16,1,4096]{2,1,0:T(1,128)S(1)} async-done(((f32[16,1,4096]{2,1,0:T(1,128)}), f32[16,1,4096]{2,1,0:T(1,128)S(1)}, u32[]{:S(2)}, u32[]{:S(2)}) %all-to-all-start.1) | async-done | bytes 262176 | tf_op jit(solution)/shard_map/all_to_all | solution.py:178
  102.7 0.5 broadcast.407
  103.2 1.3 %reduce = f32[16,4096]{1,0:T(8,128)S(1)} reduce(f32[16,1,4096]{2,1,0:T(1,128)S(1)} %all-to-all-done.1, f32[]{:T(128)} %broadcast.407), dimensions={1}, to_apply=%all_to_all.11.reduce_sub_computation | reduce | bytes 524292 | tf_op jit(solution)/shard_map/all_to_all | solution.py:178
  104.5 0.2 reshape.175
  104.7 0.1 copy.12
  104.8 0.6 fusion.56
  105.4 0.7 multiply_reduce_fusion
  106.8 0.3 fusion.9
  107.1 0.3 fusion.37
  107.3 0.2 fusion.32
  107.5 0.2 fusion.8
  107.7 0.2 fusion.60
  108.0 0.2 fusion.59
  108.2 0.2 fusion.7
  108.4 0.2 fusion.61
  108.6 0.2 fusion.62
  108.8 0.2 fusion.6
  109.0 0.3 fusion.63
  109.3 0.1 fusion.54
  109.4 0.1 slice_bitcast_fusion
  109.5 0.3 convolution_bitcast_fusion.1
  109.8 0.3 convolution_bitcast_fusion
  110.7 0.7 fusion.10
  111.4 6.3 %shard_map.60 = bf16[128,8192]{1,0:T(8,128)(2,1)} custom-call(bf16[2,128,256]{2,1,0:T(8,128)(2,1)} %get-tuple-element.11.c_hi_ref, bf16[2,128,256]{2,1,0:T(8,128)(2,1)} %get-tuple-element.10.c_lo_ref, bf16[256,4096]{1,0:T(8,128)(2,1)} %get-tuple-element.7.hi_ref, bf16[256,4096]{1,0:T(8,128)(2,1)} %get-tuple-element.6.lo_ref), custom_call_target="tpu_custom_call" | custom-call | flops 1610612736 | bytes 10485760 | tf_op jit(solution)/shard_map/pallas_call | solution.py:102
  (8 shorter events, 0.2 us)
Async XLA Ops:
  7.2 10.6 %copy-start = (f32[8192]{0:T(1024)S(1)}, f32[8192]{0:T(1024)}, u32[]{:S(2)}) copy-start(f32[8192]{0:T(1024)} %param.5) | copy-start | bytes 98308
  7.2 59.5 %all-to-all-start = ((f16[32,8,4096]{2,1,0:T(8,128)(2,1)}), f16[32,8,4096]{2,1,0:T(8,128)(2,1)S(1)}, u32[]{:S(2)}, u32[]{:S(2)}) async-start(f16[32,8,4096]{2,1,0:T(8,128)(2,1)} %fusion.1), calls=%async_computation | async-start | bytes 4194304 | tf_op jit(solution)/shard_map/all_to_all | solution.py:157
  75.7 15.4 %copy-start.1 = (s32[32]{0:T(128)S(1)}, s32[32]{0:T(128)}, u32[]{:S(2)}) copy-start(s32[32]{0:T(128)} %param.7) | copy-start | bytes 388
  78.6 24.1 %all-to-all-start.1 = ((f32[16,1,4096]{2,1,0:T(1,128)}), f32[16,1,4096]{2,1,0:T(1,128)S(1)}, u32[]{:S(2)}, u32[]{:S(2)}) async-start(f32[16,1,4096]{2,1,0:T(1,128)} %reshape.174), calls=%async_computation.1 | async-start | bytes 524288 | tf_op jit(solution)/shard_map/all_to_all | solution.py:178

commit v6 on v5

--- a/solution.py
+++ b/solution.py
@@ -158,7 +158,7 @@
     high, low = split_pair(received.astype(jnp.float32))
     recv_rows = received.shape[0]
 
-    square = gram_call(high, low, weights, 1024, 2 * local_blocks) * (1.0 / (LINK_SCALE * LINK_SCALE * total_points))
+    square = gram_call(high, low, weights, 2048, 2 * local_blocks) * (1.0 / (LINK_SCALE * LINK_SCALE * total_points))
     natural = jnp.arange(rows, dtype=jnp.int32)
     part, block = natural // block_count, natural % block_count
     group = 2 * local_blocks
@@ -172,15 +172,12 @@
     square = jnp.dot(jnp.dot(either, square, precision=HIGH), either.T, precision=HIGH)
     g_one = square[:block_count, :block_count] + square[block_count:, block_count:]
     g_two = square[:block_count, block_count:] - square[block_count:, :block_count]
-    lower = jnp.arange(block_count)[:, None] > jnp.arange(block_count)[None, :]
-    packed = jnp.where(lower, g_two, g_one)
-    spread = jnp.broadcast_to(packed[None], (space_count, block_count, block_count))
+    packed = jnp.concatenate([g_one, g_two], axis=1)
+    spread = jnp.broadcast_to(packed[None], (space_count,) + packed.shape)
     partials = lax.all_to_all(spread, "space", split_axis=0, concat_axis=0, tiled=True)
     total = jnp.sum(partials, axis=0)
-    upper = jnp.where(lower, jnp.zeros_like(total), total)
-    strict = jnp.where(lower, total, jnp.zeros_like(total))
-    g_one = upper + jnp.where(lower, upper.T, jnp.zeros_like(total))
-    g_two = strict - strict.T
+    g_one = total[:, :block_count]
+    g_two = total[:, block_count:]
 
     embedded = jnp.concatenate(
         [jnp.concatenate([g_one, -g_two], axis=1), jnp.concatenate([g_two, g_one], axis=1)], axis=0

time: 119 us -> 122 us (1.025)
  waiting for transfers between devices: 58.6 us -> 64.2 us
    all_to_all x1, waiting for transfers between devices: 10.3 us -> 16 us  [shards(): lax.all_to_all(spread, 'space', split_axis=0, concat_axis=0, tiled=True)]
    all_to_all x1 -> x0, other arithmetic: 1.26 us -> none  [shards(): lax.all_to_all(spread, 'space', split_axis=0, concat_axis=0, tiled=True)]
    unnamed x6 -> x4, local copies, waits for them, and re-layouts: 1.25 us -> 0.01 us
where the time goes in v6:
time: 122 us
  waiting for transfers between devices  64.2 us (53%)
  starting transfers between devices  23.1 us (19%)
  Pallas kernels  12 us (10%)
  other arithmetic  7.65 us (6%)
  matrix products  6.73 us (6%)
  local copies, waits for them, and re-layouts  4.04 us (3%)
  between operations  3.99 us (3%)
    all_to_all x1, waiting for transfers between devices, shards(): lax.all_to_all(sent, 'tm', split_axis=0, concat_axis=0, tiled=True)  48.3 us
    all_to_all x1, waiting for transfers between devices, shards(): lax.all_to_all(spread, 'space', split_axis=0, concat_axis=0, tiled=True)  16 us
    all_to_all x1, starting transfers between devices, shards(): lax.all_to_all(spread, 'space', split_axis=0, concat_axis=0, tiled=True)  12.5 us
    all_to_all x1, starting transfers between devices, shards(): lax.all_to_all(sent, 'tm', split_axis=0, concat_axis=0, tiled=True)  10.6 us
    pallas_call x1, Pallas kernels, mode_call(): pl.pallas_call(mode_kernel, grid=(halves, steps), in_specs=[pl.BlockSpec(...  6.3 us
    pallas_call x1, Pallas kernels, gram_call(): pl.pallas_call(functools.partial(gram_kernel, group), grid=(points // chu...  5.75 us
    convert_element_type x2, other arithmetic, split_pair(): (value - rounded).astype(jnp.bfloat16)  3.49 us
  transfers between devices with their start and end apart: 2, of which 2 were waited for; matrix products, arithmetic and copies ran while one was open for 2% of the time, Pallas kernels for 0%

profile of v6, /device:TPU:1, one launch (start us, length us, event | category | flops | bytes accessed | tf_op | source)
XLA Modules:
  0.0 121.8 jit_solution(16753495203347592986)
XLA Ops:
  0.6 0.6 multiply_reduce_fusion.1
  2.0 0.8 divide_convert_fusion.1
  2.9 0.1 broadcast_multiply_fusion.1
  3.0 0.3 broadcast_multiply_fusion
  3.3 0.2 mul.187
  3.5 1.7 %fusion.51 = (bf16[128,4096]{1,0:T(8,128)(2,1)S(1)}, bf16[128,4096]{1,0:T(8,128)(2,1)S(1)}) fusion(bf16[128,8192]{1,0:T(8,128)(2,1)} %param.4), kind=kLoop, calls=%fused_computation.104 | loop fusion | bytes 4194304 | tf_op jit(solution)/shard_map/slice | solution.py:40
  5.2 2.1 %fusion.1 = f16[32,8,4096]{2,1,0:T(8,128)(2,1)} fusion(bf16[256,256]{1,0:T(8,128)(2,1)S(1)} %mul.187, bf16[128,4096]{1,0:T(8,128)(2,1)S(1)} %get-tuple-element.5, bf16[128,4096]{1,0:T(8,128)(2,1)S(1)} %get-tuple-element.4), kind=kOutput, calls=%fused_computation.4 | convolution fusion | flops 543162368 | bytes 4325376 | tf_op jit(solution)/shard_map/dot_general | solution.py:41
  7.2 0.0 copy-start
  7.2 10.6 %all-to-all-start = ((f16[32,8,4096]{2,1,0:T(8,128)(2,1)}), f16[32,8,4096]{2,1,0:T(8,128)(2,1)S(1)}, u32[]{:S(2)}, u32[]{:S(2)}) async-start(f16[32,8,4096]{2,1,0:T(8,128)(2,1)} %fusion.1), calls=%async_computation | async-start | bytes 4194304 | tf_op jit(solution)/shard_map/all_to_all | solution.py:157
  17.9 0.0 copy-done
  17.9 0.6 reshape.170.w_ref
  18.5 48.3 %all-to-all-done = f16[32,8,4096]{2,1,0:T(8,128)(2,1)S(1)} async-done(((f16[32,8,4096]{2,1,0:T(8,128)(2,1)}), f16[32,8,4096]{2,1,0:T(8,128)(2,1)S(1)}, u32[]{:S(2)}, u32[]{:S(2)}) %all-to-all-start) | async-done | bytes 2097184 | tf_op jit(solution)/shard_map/all_to_all | solution.py:157
  66.8 2.8 %fusion.2 = (bf16[256,4096]{1,0:T(8,128)(2,1)}, bf16[256,4096]{1,0:T(8,128)(2,1)}) fusion(f16[32,8,4096]{2,1,0:T(8,128)(2,1)S(1)} %all-to-all-done), kind=kLoop, calls=%fused_computation.5 | loop fusion | flops 5242880 | bytes 6291456 | tf_op jit(solution)/shard_map/convert_element_type | solution.py:46
  69.5 5.7 %shard_map.59 = f32[256,256]{1,0:T(8,128)} custom-call(bf16[256,4096]{1,0:T(8,128)(2,1)} %get-tuple-element.3.hi_ref, bf16[256,4096]{1,0:T(8,128)(2,1)} %get-tuple-element.2.lo_ref, f32[2,4096]{1,0:T(2,128)} %reshape.170.w_ref), custom_call_target="tpu_custom_call" | custom-call | flops 1610612736 | bytes 4194304 | tf_op jit(solution)/shard_map/pallas_call | solution.py:71
  75.3 0.0 copy-start.1
  75.3 1.4 %fusion.11 = f32[128,256]{1,0:T(8,128)S(1)} fusion(f32[256,256]{1,0:T(8,128)} %shard_map.59, s32[256]{0:T(256)S(1)} %and_select_fusion, s32[128]{0:T(128)S(1)} %get-tuple-element.21, s32[128]{0:T(128)S(1)} %get-tuple-element.20), kind=kOutput, calls=%fused_computation.23 | convolution fusion | flops 101023744 | bytes 395264 | tf_op jit(solution)/shard_map/dot_general | solution.py:172
  76.6 0.4 fusion.18
  77.0 0.1 slice_add_fusion
  77.1 0.1 pad_maximum_fusion.1
  77.2 0.9 broadcast_in_dim.14
  78.0 12.5 %all-to-all-start.1 = ((f32[16,64,128]{2,1,0:T(8,128)}), f32[16,64,128]{2,1,0:T(8,128)S(1)}, u32[]{:S(2)}, u32[]{:S(2)}) async-start(f32[16,64,128]{2,1,0:T(8,128)} %broadcast_in_dim.14), calls=%async_computation.1 | async-start | bytes 1048576 | tf_op jit(solution)/shard_map/all_to_all | solution.py:177
  90.5 0.0 copy-done.1
  90.5 0.6 dynamic_slice.3
  91.1 0.7 broadcast_compare_fusion
  91.8 16.0 %all-to-all-done.1 = f32[16,64,128]{2,1,0:T(8,128)S(1)} async-done(((f32[16,64,128]{2,1,0:T(8,128)}), f32[16,64,128]{2,1,0:T(8,128)S(1)}, u32[]{:S(2)}, u32[]{:S(2)}) %all-to-all-start.1) | async-done | bytes 524320 | tf_op jit(solution)/shard_map/all_to_all | solution.py:177
  107.8 0.6 select_reduce_fusion
  108.4 0.7 multiply_reduce_fusion
  109.8 0.3 fusion.9
  110.0 0.3 fusion.33
  110.3 0.2 fusion.32
  110.5 0.2 fusion.8
  110.7 0.2 fusion.53
  110.9 0.2 fusion.52
  111.1 0.2 fusion.7
  111.3 0.2 fusion.54
  111.6 0.2 fusion.55
  111.8 0.2 fusion.6
  112.0 0.3 fusion.56
  112.3 0.1 fusion.50
  112.3 0.1 slice_bitcast_fusion
  112.4 0.3 convolution_bitcast_fusion.1
  112.7 0.3 convolution_bitcast_fusion
  113.6 0.7 fusion.10
  114.4 6.3 %shard_map.60 = bf16[128,8192]{1,0:T(8,128)(2,1)} custom-call(bf16[2,128,256]{2,1,0:T(8,128)(2,1)} %get-tuple-element.7.c_hi_ref, bf16[2,128,256]{2,1,0:T(8,128)(2,1)} %get-tuple-element.6.c_lo_ref, bf16[256,4096]{1,0:T(8,128)(2,1)} %get-tuple-element.3.hi_ref, bf16[256,4096]{1,0:T(8,128)(2,1)} %get-tuple-element.2.lo_ref), custom_call_target="tpu_custom_call" | custom-call | flops 1610612736 | bytes 10485760 | tf_op jit(solution)/shard_map/pallas_call | solution.py:102
  (7 shorter events, 0.1 us)
Async XLA Ops:
  7.2 10.6 %copy-start = (f32[8192]{0:T(1024)S(1)}, f32[8192]{0:T(1024)}, u32[]{:S(2)}) copy-start(f32[8192]{0:T(1024)} %param.5) | copy-start | bytes 98308
  7.2 59.5 %all-to-all-start = ((f16[32,8,4096]{2,1,0:T(8,128)(2,1)}), f16[32,8,4096]{2,1,0:T(8,128)(2,1)S(1)}, u32[]{:S(2)}, u32[]{:S(2)}) async-start(f16[32,8,4096]{2,1,0:T(8,128)(2,1)} %fusion.1), calls=%async_computation | async-start | bytes 4194304 | tf_op jit(solution)/shard_map/all_to_all | solution.py:157
  75.3 15.3 %copy-start.1 = (s32[32]{0:T(128)S(1)}, s32[32]{0:T(128)}, u32[]{:S(2)}) copy-start(s32[32]{0:T(128)} %param.7) | copy-start | bytes 388
  78.0 29.7 %all-to-all-start.1 = ((f32[16,64,128]{2,1,0:T(8,128)}), f32[16,64,128]{2,1,0:T(8,128)S(1)}, u32[]{:S(2)}, u32[]{:S(2)}) async-start(f32[16,64,128]{2,1,0:T(8,128)} %broadcast_in_dim.14), calls=%async_computation.1 | async-start | bytes 1048576 | tf_op jit(solution)/shard_map/all_to_all | solution.py:177

commit v7 on v5

--- a/solution.py
+++ b/solution.py
@@ -101,14 +101,14 @@
     c_hi, c_lo = split_pair(coeff_halves)
     return pl.pallas_call(
         mode_kernel,
-        grid=(halves, steps),
+        grid=(steps, halves),
         in_specs=[
-            pl.BlockSpec((None, out_rows, rows), lambda h, k: (h, 0, 0)),
-            pl.BlockSpec((None, out_rows, rows), lambda h, k: (h, 0, 0)),
-            pl.BlockSpec((rows, chunk), lambda h, k: (0, k)),
-            pl.BlockSpec((rows, chunk), lambda h, k: (0, k)),
+            pl.BlockSpec((None, out_rows, rows), lambda k, h: (h, 0, 0)),
+            pl.BlockSpec((None, out_rows, rows), lambda k, h: (h, 0, 0)),
+            pl.BlockSpec((rows, chunk), lambda k, h: (0, k)),
+            pl.BlockSpec((rows, chunk), lambda k, h: (0, k)),
         ],
-        out_specs=pl.BlockSpec((out_rows, chunk), lambda h, k: (0, h * steps + k)),
+        out_specs=pl.BlockSpec((out_rows, chunk), lambda k, h: (0, h * steps + k)),
         out_shape=jax.ShapeDtypeStruct((out_rows, halves * points), jnp.bfloat16),
         cost_estimate=pl.CostEstimate(
             flops=6 * out_rows * rows * points * halves,
@@ -132,8 +132,10 @@
     frobenius = jnp.sqrt(jnp.sum(embedded * embedded) + 1e-06)
     identity = jnp.eye(size_two, dtype=jnp.float32)
     current = embedded / frobenius
-    result = identity
-    for sweep in range(NS_STEPS):
+    factor = 1.5 * identity - 0.5 * current
+    current = jnp.dot(current, factor, precision=HIGH)
+    result = factor
+    for sweep in range(1, NS_STEPS):
         factor = 1.5 * identity - 0.5 * jnp.dot(result, current, precision=HIGH)
         current = jnp.dot(current, factor, precision=HIGH)
         result = jnp.dot(factor, result, precision=HIGH)
@@ -158,7 +160,7 @@
     high, low = split_pair(received.astype(jnp.float32))
     recv_rows = received.shape[0]
 
-    square = gram_call(high, low, weights, 1024, 2 * local_blocks) * (1.0 / (LINK_SCALE * LINK_SCALE * total_points))
+    square = gram_call(high, low, weights, 2048, 2 * local_blocks) * (1.0 / (LINK_SCALE * LINK_SCALE * total_points))
     natural = jnp.arange(rows, dtype=jnp.int32)
     part, block = natural // block_count, natural % block_count
     group = 2 * local_blocks

time: 119 us -> 119 us (level)
  no operation moved by 1% of the time
where the time goes in v7:
time: 119 us; the launch traced here: 118 us
  waiting for transfers between devices  58.6 us (49%)
  starting transfers between devices  23.1 us (19%)
  Pallas kernels  12 us (10%)
  other arithmetic  8.87 us (7%)
  matrix products  6.45 us (5%)
  local copies, waits for them, and re-layouts  5.07 us (4%)
  between operations  4.01 us (3%)
    all_to_all x1, waiting for transfers between devices, shards(): lax.all_to_all(sent, 'tm', split_axis=0, concat_axis=0, tiled=True)  48.3 us
    all_to_all x1, starting transfers between devices, shards(): lax.all_to_all(spread, 'space', split_axis=0, concat_axis=0, tiled=True)  12.5 us
    all_to_all x1, starting transfers between devices, shards(): lax.all_to_all(sent, 'tm', split_axis=0, concat_axis=0, tiled=True)  10.6 us
    all_to_all x1, waiting for transfers between devices, shards(): lax.all_to_all(spread, 'space', split_axis=0, concat_axis=0, tiled=True)  10.3 us
    pallas_call x1, Pallas kernels, mode_call(): pl.pallas_call(mode_kernel, grid=(steps, halves), in_specs=[pl.BlockSpec(...  6.24 us
    pallas_call x1, Pallas kernels, gram_call(): pl.pallas_call(functools.partial(gram_kernel, group), grid=(points // chu...  5.74 us
    convert_element_type x2, other arithmetic, split_pair(): (value - rounded).astype(jnp.bfloat16)  3.51 us
  transfers between devices with their start and end apart: 2, of which 2 were waited for; matrix products, arithmetic and copies ran while one was open for 2% of the time, Pallas kernels for 0%

profile of v7, /device:TPU:1, one launch (start us, length us, event | category | flops | bytes accessed | tf_op | source)
XLA Modules:
  0.0 118.1 jit_solution(3252389633019066819)
XLA Ops:
  0.6 0.6 multiply_reduce_fusion.1
  2.0 0.8 divide_convert_fusion.1
  2.9 0.1 broadcast_multiply_fusion.1
  3.0 0.3 broadcast_multiply_fusion
  3.3 0.2 mul.187
  3.5 1.7 %fusion.75 = (bf16[128,4096]{1,0:T(8,128)(2,1)S(1)}, bf16[128,4096]{1,0:T(8,128)(2,1)S(1)}) fusion(bf16[128,8192]{1,0:T(8,128)(2,1)} %param.4), kind=kLoop, calls=%fused_computation.128 | loop fusion | bytes 4194304 | tf_op jit(solution)/shard_map/slice | solution.py:40
  5.2 2.1 %fusion.1 = f16[32,8,4096]{2,1,0:T(8,128)(2,1)} fusion(bf16[256,256]{1,0:T(8,128)(2,1)S(1)} %mul.187, bf16[128,4096]{1,0:T(8,128)(2,1)S(1)} %get-tuple-element.9, bf16[128,4096]{1,0:T(8,128)(2,1)S(1)} %get-tuple-element.8), kind=kOutput, calls=%fused_computation.4 | convolution fusion | flops 543162368 | bytes 4325376 | tf_op jit(solution)/shard_map/dot_general | solution.py:41
  7.2 0.0 copy-start
  7.2 10.6 %all-to-all-start = ((f16[32,8,4096]{2,1,0:T(8,128)(2,1)}), f16[32,8,4096]{2,1,0:T(8,128)(2,1)S(1)}, u32[]{:S(2)}, u32[]{:S(2)}) async-start(f16[32,8,4096]{2,1,0:T(8,128)(2,1)} %fusion.1), calls=%async_computation | async-start | bytes 4194304 | tf_op jit(solution)/shard_map/all_to_all | solution.py:159
  17.9 0.0 copy-done
  17.9 0.6 reshape.170.w_ref
  18.5 48.3 %all-to-all-done = f16[32,8,4096]{2,1,0:T(8,128)(2,1)S(1)} async-done(((f16[32,8,4096]{2,1,0:T(8,128)(2,1)}), f16[32,8,4096]{2,1,0:T(8,128)(2,1)S(1)}, u32[]{:S(2)}, u32[]{:S(2)}) %all-to-all-start) | async-done | bytes 2097184 | tf_op jit(solution)/shard_map/all_to_all | solution.py:159
  66.8 2.8 %fusion.2 = (bf16[256,4096]{1,0:T(8,128)(2,1)}, bf16[256,4096]{1,0:T(8,128)(2,1)}) fusion(f16[32,8,4096]{2,1,0:T(8,128)(2,1)S(1)} %all-to-all-done), kind=kLoop, calls=%fused_computation.5 | loop fusion | flops 5242880 | bytes 6291456 | tf_op jit(solution)/shard_map/convert_element_type | solution.py:46
  69.6 5.7 %shard_map.59 = f32[256,256]{1,0:T(8,128)} custom-call(bf16[256,4096]{1,0:T(8,128)(2,1)} %get-tuple-element.7.hi_ref, bf16[256,4096]{1,0:T(8,128)(2,1)} %get-tuple-element.6.lo_ref, f32[2,4096]{1,0:T(2,128)} %reshape.170.w_ref), custom_call_target="tpu_custom_call" | custom-call | flops 1610612736 | bytes 4194304 | tf_op jit(solution)/shard_map/pallas_call | solution.py:71
  75.3 0.0 copy-start.1
  75.3 1.4 %fusion.10 = f32[128,256]{1,0:T(8,128)S(1)} fusion(f32[256,256]{1,0:T(8,128)} %shard_map.59, s32[256]{0:T(256)S(1)} %and_select_fusion, s32[128]{0:T(128)S(1)} %get-tuple-element.21, s32[128]{0:T(128)S(1)} %get-tuple-element.20), kind=kOutput, calls=%fused_computation.21 | convolution fusion | flops 101023744 | bytes 395264 | tf_op jit(solution)/shard_map/dot_general | solution.py:174
  76.7 0.4 fusion.17
  77.0 0.1 fusion.33
  77.2 1.0 reshape.174
  78.2 12.5 %all-to-all-start.1 = ((f32[16,1,4096]{2,1,0:T(1,128)}), f32[16,1,4096]{2,1,0:T(1,128)S(1)}, u32[]{:S(2)}, u32[]{:S(2)}) async-start(f32[16,1,4096]{2,1,0:T(1,128)} %reshape.174), calls=%async_computation.1 | async-start | bytes 524288 | tf_op jit(solution)/shard_map/all_to_all | solution.py:180
  90.7 0.0 copy-done.1
  90.7 0.6 dynamic_slice.3
  91.3 0.7 broadcast_compare_fusion
  92.0 10.3 %all-to-all-done.1 = f32[16,1,4096]{2,1,0:T(1,128)S(1)} async-done(((f32[16,1,4096]{2,1,0:T(1,128)}), f32[16,1,4096]{2,1,0:T(1,128)S(1)}, u32[]{:S(2)}, u32[]{:S(2)}) %all-to-all-start.1) | async-done | bytes 262176 | tf_op jit(solution)/shard_map/all_to_all | solution.py:180
  102.3 0.5 broadcast.437
  102.8 1.3 %reduce = f32[16,4096]{1,0:T(8,128)S(1)} reduce(f32[16,1,4096]{2,1,0:T(1,128)S(1)} %all-to-all-done.1, f32[]{:T(128)} %broadcast.437), dimensions={1}, to_apply=%all_to_all.11.reduce_sub_computation | reduce | bytes 524292 | tf_op jit(solution)/shard_map/all_to_all | solution.py:180
  104.1 0.2 reshape.175
  104.3 0.1 copy.12
  104.4 0.6 fusion.73
  105.1 0.7 multiply_reduce_fusion
  106.4 0.3 fusion.26
  106.7 0.3 fusion.8
  107.0 0.3 fusion.25
  107.3 0.2 fusion.76
  107.5 0.2 fusion.7
  107.7 0.2 fusion.77
  107.9 0.2 fusion.78
  108.1 0.2 fusion.6
  108.3 0.3 fusion.79
  108.6 0.1 fusion.71
  108.7 0.1 slice_bitcast_fusion
  108.8 0.3 convolution_bitcast_fusion.1
  109.1 0.3 convolution_bitcast_fusion
  110.0 0.7 fusion.9
  110.7 6.2 %shard_map.60 = bf16[128,8192]{1,0:T(8,128)(2,1)} custom-call(bf16[2,128,256]{2,1,0:T(8,128)(2,1)} %get-tuple-element.11.c_hi_ref, bf16[2,128,256]{2,1,0:T(8,128)(2,1)} %get-tuple-element.10.c_lo_ref, bf16[256,4096]{1,0:T(8,128)(2,1)} %get-tuple-element.7.hi_ref, bf16[256,4096]{1,0:T(8,128)(2,1)} %get-tuple-element.6.lo_ref), custom_call_target="tpu_custom_call" | custom-call | flops 1610612736 | bytes 10485760 | tf_op jit(solution)/shard_map/pallas_call | solution.py:102
  (8 shorter events, 0.2 us)
Async XLA Ops:
  7.2 10.6 %copy-start = (f32[8192]{0:T(1024)S(1)}, f32[8192]{0:T(1024)}, u32[]{:S(2)}) copy-start(f32[8192]{0:T(1024)} %param.5) | copy-start | bytes 98308
  7.2 59.5 %all-to-all-start = ((f16[32,8,4096]{2,1,0:T(8,128)(2,1)}), f16[32,8,4096]{2,1,0:T(8,128)(2,1)S(1)}, u32[]{:S(2)}, u32[]{:S(2)}) async-start(f16[32,8,4096]{2,1,0:T(8,128)(2,1)} %fusion.1), calls=%async_computation | async-start | bytes 4194304 | tf_op jit(solution)/shard_map/all_to_all | solution.py:159
  75.3 15.4 %copy-start.1 = (s32[32]{0:T(128)S(1)}, s32[32]{0:T(128)}, u32[]{:S(2)}) copy-start(s32[32]{0:T(128)} %param.7) | copy-start | bytes 388
  78.2 24.1 %all-to-all-start.1 = ((f32[16,1,4096]{2,1,0:T(1,128)}), f32[16,1,4096]{2,1,0:T(1,128)S(1)}, u32[]{:S(2)}, u32[]{:S(2)}) async-start(f32[16,1,4096]{2,1,0:T(1,128)} %reshape.174), calls=%async_computation.1 | async-start | bytes 524288 | tf_op jit(solution)/shard_map/all_to_all | solution.py:180

commit v8 on v7

--- a/solution.py
+++ b/solution.py
@@ -176,9 +176,14 @@
     g_two = square[:block_count, block_count:] - square[block_count:, :block_count]
     lower = jnp.arange(block_count)[:, None] > jnp.arange(block_count)[None, :]
     packed = jnp.where(lower, g_two, g_one)
-    spread = jnp.broadcast_to(packed[None], (space_count, block_count, block_count))
+    rows_half = block_count // 2
+    packed = jnp.concatenate([packed[:rows_half], packed[rows_half:]], axis=1)
+    spread = jnp.broadcast_to(packed[None], (space_count,) + packed.shape)
     partials = lax.all_to_all(spread, "space", split_axis=0, concat_axis=0, tiled=True)
-    total = jnp.sum(partials, axis=0)
+    total = partials[0]
+    for source in range(1, space_count):
+        total = total + partials[source]
+    total = jnp.concatenate([total[:, :block_count], total[:, block_count:]], axis=0)
     upper = jnp.where(lower, jnp.zeros_like(total), total)
     strict = jnp.where(lower, total, jnp.zeros_like(total))
     g_one = upper + jnp.where(lower, upper.T, jnp.zeros_like(total))

time: 119 us -> 118 us (level)
    all_to_all x1 -> x0, other arithmetic: 1.26 us -> none  [shards(): lax.all_to_all(spread, 'space', split_axis=0, concat_axis=0, tiled=True)]
where the time goes in v8:
time: 118 us
  waiting for transfers between devices  58.5 us (50%)
  starting transfers between devices  23.1 us (20%)
  Pallas kernels  12 us (10%)
  other arithmetic  7.8 us (7%)
  matrix products  6.44 us (5%)
  local copies, waits for them, and re-layouts  5.83 us (5%)
  between operations  4.1 us (3%)
    all_to_all x1, waiting for transfers between devices, shards(): lax.all_to_all(sent, 'tm', split_axis=0, concat_axis=0, tiled=True)  48.2 us
    all_to_all x1, starting transfers between devices, shards(): lax.all_to_all(spread, 'space', split_axis=0, concat_axis=0, tiled=True)  12.5 us
    all_to_all x1, starting transfers between devices, shards(): lax.all_to_all(sent, 'tm', split_axis=0, concat_axis=0, tiled=True)  10.6 us
    all_to_all x1, waiting for transfers between devices, shards(): lax.all_to_all(spread, 'space', split_axis=0, concat_axis=0, tiled=True)  10.2 us
    pallas_call x1, Pallas kernels, mode_call(): pl.pallas_call(mode_kernel, grid=(steps, halves), in_specs=[pl.BlockSpec(...  6.24 us
    pallas_call x1, Pallas kernels, gram_call(): pl.pallas_call(functools.partial(gram_kernel, group), grid=(points // chu...  5.76 us
    convert_element_type x2, other arithmetic, split_pair(): (value - rounded).astype(jnp.bfloat16)  3.49 us
  transfers between devices with their start and end apart: 2, of which 2 were waited for; matrix products, arithmetic and copies ran while one was open for 2% of the time, Pallas kernels for 0%

profile of v8, /device:TPU:1, one launch (start us, length us, event | category | flops | bytes accessed | tf_op | source)
XLA Modules:
  0.0 117.8 jit_solution(6888219664247109953)
XLA Ops:
  0.6 0.6 multiply_reduce_fusion.1
  2.0 0.8 divide_convert_fusion.1
  2.9 0.1 broadcast_multiply_fusion.1
  3.0 0.3 broadcast_multiply_fusion
  3.3 0.2 mul.187
  3.5 1.7 %fusion.73 = (bf16[128,4096]{1,0:T(8,128)(2,1)S(1)}, bf16[128,4096]{1,0:T(8,128)(2,1)S(1)}) fusion(bf16[128,8192]{1,0:T(8,128)(2,1)} %param.4), kind=kLoop, calls=%fused_computation.130 | loop fusion | bytes 4194304 | tf_op jit(solution)/shard_map/slice | solution.py:40
  5.2 2.1 %fusion.1 = f16[32,8,4096]{2,1,0:T(8,128)(2,1)} fusion(bf16[256,256]{1,0:T(8,128)(2,1)S(1)} %mul.187, bf16[128,4096]{1,0:T(8,128)(2,1)S(1)} %get-tuple-element.11, bf16[128,4096]{1,0:T(8,128)(2,1)S(1)} %get-tuple-element.10), kind=kOutput, calls=%fused_computation.4 | convolution fusion | flops 543162368 | bytes 4325376 | tf_op jit(solution)/shard_map/dot_general | solution.py:41
  7.2 10.6 %all-to-all-start = ((f16[32,8,4096]{2,1,0:T(8,128)(2,1)}), f16[32,8,4096]{2,1,0:T(8,128)(2,1)S(1)}, u32[]{:S(2)}, u32[]{:S(2)}) async-start(f16[32,8,4096]{2,1,0:T(8,128)(2,1)} %fusion.1), calls=%async_computation | async-start | bytes 4194304 | tf_op jit(solution)/shard_map/all_to_all | solution.py:159
  17.9 0.6 reshape.174.w_ref
  18.5 48.2 %all-to-all-done = f16[32,8,4096]{2,1,0:T(8,128)(2,1)S(1)} async-done(((f16[32,8,4096]{2,1,0:T(8,128)(2,1)}), f16[32,8,4096]{2,1,0:T(8,128)(2,1)S(1)}, u32[]{:S(2)}, u32[]{:S(2)}) %all-to-all-start) | async-done | bytes 2097184 | tf_op jit(solution)/shard_map/all_to_all | solution.py:159
  66.8 2.8 %fusion.2 = (bf16[256,4096]{1,0:T(8,128)(2,1)}, bf16[256,4096]{1,0:T(8,128)(2,1)}) fusion(f16[32,8,4096]{2,1,0:T(8,128)(2,1)S(1)} %all-to-all-done), kind=kLoop, calls=%fused_computation.5 | loop fusion | flops 5242880 | bytes 6291456 | tf_op jit(solution)/shard_map/convert_element_type | solution.py:46
  69.5 5.8 %shard_map.59 = f32[256,256]{1,0:T(8,128)} custom-call(bf16[256,4096]{1,0:T(8,128)(2,1)} %get-tuple-element.9.hi_ref, bf16[256,4096]{1,0:T(8,128)(2,1)} %get-tuple-element.8.lo_ref, f32[2,4096]{1,0:T(2,128)} %reshape.174.w_ref), custom_call_target="tpu_custom_call" | custom-call | flops 1610612736 | bytes 4194304 | tf_op jit(solution)/shard_map/pallas_call | solution.py:71
  75.3 1.3 %fusion.10 = f32[128,256]{1,0:T(8,128)S(1)} fusion(f32[256,256]{1,0:T(8,128)} %shard_map.59, s32[256]{0:T(256)S(1)} %and_select_fusion, s32[128]{0:T(128)S(1)} %get-tuple-element.41, s32[128]{0:T(128)S(1)} %get-tuple-element.40), kind=kOutput, calls=%fused_computation.21 | convolution fusion | flops 101023744 | bytes 395264 | tf_op jit(solution)/shard_map/dot_general | solution.py:174
  76.6 0.4 fusion.17
  77.2 0.7 broadcast_in_dim.12
  77.9 12.5 %all-to-all-start.1 = ((f32[16,32,128]{2,1,0:T(8,128)}), f32[16,32,128]{2,1,0:T(8,128)S(1)}, u32[]{:S(2)}, u32[]{:S(2)}) async-start(f32[16,32,128]{2,1,0:T(8,128)} %broadcast_in_dim.12), calls=%async_computation.1 | async-start | bytes 524288 | tf_op jit(solution)/shard_map/all_to_all | solution.py:182
  90.5 0.6 dynamic_slice.3
  91.1 0.7 broadcast_compare_fusion
  91.8 10.2 %all-to-all-done.1 = f32[16,32,128]{2,1,0:T(8,128)S(1)} async-done(((f32[16,32,128]{2,1,0:T(8,128)}), f32[16,32,128]{2,1,0:T(8,128)S(1)}, u32[]{:S(2)}, u32[]{:S(2)}) %all-to-all-start.1) | async-done | bytes 262176 | tf_op jit(solution)/shard_map/all_to_all | solution.py:182
  102.0 0.1 copy.36
  102.2 0.1 copy.48
  102.3 0.1 copy.47
  102.4 0.1 copy.46
  102.5 0.1 copy.45
  102.6 0.1 copy.44
  102.7 0.1 copy.43
  102.8 0.1 copy.42
  102.9 0.1 copy.41
  103.0 0.1 copy.40
  103.1 0.1 copy.39
  103.2 0.1 copy.38
  103.3 0.1 copy.37
  103.5 0.1 copy.50
  104.1 0.6 select_reduce_fusion
  104.7 0.7 multiply_reduce_fusion
  106.1 0.3 fusion.26
  106.4 0.3 fusion.8
  106.6 0.3 fusion.25
  106.9 0.2 fusion.77
  107.1 0.2 fusion.7
  107.4 0.2 fusion.78
  107.6 0.2 fusion.79
  107.8 0.2 fusion.6
  108.0 0.3 fusion.80
  108.4 0.3 convolution_bitcast_fusion.1
  108.7 0.3 convolution_bitcast_fusion
  109.7 0.7 fusion.9
  110.4 6.2 %shard_map.60 = bf16[128,8192]{1,0:T(8,128)(2,1)} custom-call(bf16[2,128,256]{2,1,0:T(8,128)(2,1)} %get-tuple-element.13.c_hi_ref, bf16[2,128,256]{2,1,0:T(8,128)(2,1)} %get-tuple-element.12.c_lo_ref, bf16[256,4096]{1,0:T(8,128)(2,1)} %get-tuple-element.9.hi_ref, bf16[256,4096]{1,0:T(8,128)(2,1)} %get-tuple-element.8.lo_ref), custom_call_target="tpu_custom_call" | custom-call | flops 1610612736 | bytes 10485760 | tf_op jit(solution)/shard_map/pallas_call | solution.py:102
  (28 shorter events, 1.1 us)
Async XLA Ops:
  7.2 10.6 %copy-start = (f32[8192]{0:T(1024)S(1)}, f32[8192]{0:T(1024)}, u32[]{:S(2)}) copy-start(f32[8192]{0:T(1024)} %param.5) | copy-start | bytes 98308
  7.2 59.5 %all-to-all-start = ((f16[32,8,4096]{2,1,0:T(8,128)(2,1)}), f16[32,8,4096]{2,1,0:T(8,128)(2,1)S(1)}, u32[]{:S(2)}, u32[]{:S(2)}) async-start(f16[32,8,4096]{2,1,0:T(8,128)(2,1)} %fusion.1), calls=%async_computation | async-start | bytes 4194304 | tf_op jit(solution)/shard_map/all_to_all | solution.py:159
  69.5 21.0 %copy-start.1 = (s32[32]{0:T(128)S(1)}, s32[32]{0:T(128)}, u32[]{:S(2)}) copy-start(s32[32]{0:T(128)} %param.7) | copy-start | bytes 388
  77.9 24.1 %all-to-all-start.1 = ((f32[16,32,128]{2,1,0:T(8,128)}), f32[16,32,128]{2,1,0:T(8,128)S(1)}, u32[]{:S(2)}, u32[]{:S(2)}) async-start(f32[16,32,128]{2,1,0:T(8,128)} %broadcast_in_dim.12), calls=%async_computation.1 | async-start | bytes 524288 | tf_op jit(solution)/shard_map/all_to_all | solution.py:182

commit v9 on v8

--- a/solution.py
+++ b/solution.py
@@ -25,9 +25,10 @@
     return jnp.concatenate([real_rows, imag_rows], axis=0).astype(jnp.bfloat16)
 
 
-def transform_blocks(dft_table, snapshots, freq_count, halves):
+def transform_blocks(dft_table, snapshots, freq_count, halves, chunks):
     local_blocks = snapshots.shape[0] // NT
     points = snapshots.shape[1] // halves
+    width = points // chunks
     table_view = dft_table.reshape(2, freq_count, NT).transpose(1, 0, 2)
     chooser = jnp.eye(local_blocks, dtype=dft_table.dtype)
     halver = jnp.eye(halves, dtype=dft_table.dtype)
@@ -37,8 +38,13 @@
         * chooser[None, None, None, :, None, :, None]
     )
     lifted = lifted.reshape(freq_count * halves * 2 * local_blocks, halves * local_blocks * NT)
-    stacked = jnp.concatenate([snapshots[:, h * points:(h + 1) * points] for h in range(halves)], axis=0)
-    return jnp.dot(lifted, stacked, preferred_element_type=jnp.float32)
+    out = []
+    for c in range(chunks):
+        stacked = jnp.concatenate(
+            [snapshots[:, h * points + c * width:h * points + (c + 1) * width] for h in range(halves)], axis=0
+        )
+        out.append(jnp.dot(lifted, stacked, preferred_element_type=jnp.float32))
+    return out
 
 
 def split_pair(value):
@@ -84,38 +90,47 @@
     )(high, low, weights.reshape(2, points))
 
 
-def mode_kernel(c_hi_ref, c_lo_ref, hi_ref, lo_ref, o_ref):
-    x_hi = hi_ref[...]
-    x_lo = lo_ref[...]
+def mode_kernel(c_hi_ref, c_lo_ref, *refs):
+    o_ref = refs[-1]
+    pairs = refs[:-1]
+    c = pl.program_id(0)
     c_hi = c_hi_ref[...]
-    acc = jnp.dot(c_hi, x_hi, preferred_element_type=jnp.float32)
-    acc += jnp.dot(c_lo_ref[...], x_hi, preferred_element_type=jnp.float32)
-    acc += jnp.dot(c_hi, x_lo, preferred_element_type=jnp.float32)
-    o_ref[...] = acc.astype(o_ref.dtype)
-
-
-def mode_call(coeff_halves, high, low, chunk):
+    c_lo = c_lo_ref[...]
+    for index in range(len(pairs) // 2):
+
+        @pl.when(c == index)
+        def _():
+            x_hi = pairs[2 * index][...]
+            x_lo = pairs[2 * index + 1][...]
+            acc = jnp.dot(c_hi, x_hi, preferred_element_type=jnp.float32)
+            acc += jnp.dot(c_lo, x_hi, preferred_element_type=jnp.float32)
+            acc += jnp.dot(c_hi, x_lo, preferred_element_type=jnp.float32)
+            o_ref[...] = acc.astype(o_ref.dtype)
+
+
+def mode_call(coeff_halves, pieces):
     halves, out_rows, rows = coeff_halves.shape
-    points = high.shape[1]
-    steps = points // chunk
+    chunks = len(pieces)
+    width = pieces[0][0].shape[1]
     c_hi, c_lo = split_pair(coeff_halves)
+    whole = pl.BlockSpec((rows, width), lambda c, h: (0, 0))
+    flat = [array for pair in pieces for array in pair]
     return pl.pallas_call(
         mode_kernel,
-        grid=(steps, halves),
+        grid=(chunks, halves),
         in_specs=[
-            pl.BlockSpec((None, out_rows, rows), lambda k, h: (h, 0, 0)),
-            pl.BlockSpec((None, out_rows, rows), lambda k, h: (h, 0, 0)),
-            pl.BlockSpec((rows, chunk), lambda k, h: (0, k)),
-            pl.BlockSpec((rows, chunk), lambda k, h: (0, k)),
-        ],
-        out_specs=pl.BlockSpec((out_rows, chunk), lambda k, h: (0, h * steps + k)),
-        out_shape=jax.ShapeDtypeStruct((out_rows, halves * points), jnp.bfloat16),
+            pl.BlockSpec((None, out_rows, rows), lambda c, h: (h, 0, 0)),
+            pl.BlockSpec((None, out_rows, rows), lambda c, h: (h, 0, 0)),
+        ]
+        + [whole] * len(flat),
+        out_specs=pl.BlockSpec((out_rows, width), lambda c, h: (0, h * chunks + c)),
+        out_shape=jax.ShapeDtypeStruct((out_rows, halves * chunks * width), jnp.bfloat16),
         cost_estimate=pl.CostEstimate(
-            flops=6 * out_rows * rows * points * halves,
+            flops=6 * out_rows * rows * width * chunks * halves,
             transcendentals=0,
-            bytes_accessed=4 * rows * points * halves + 2 * out_rows * points * halves,
+            bytes_accessed=4 * rows * width * chunks + 2 * out_rows * width * chunks * halves,
         ),
-    )(c_hi, c_lo, high, low)
+    )(c_hi, c_lo, *flat)
 
 
 def butterfly_sum(value, axis, size):
@@ -154,13 +169,22 @@
 
     dft_table = spectra_table(freqs)
     halves = 2
-    spectra = transform_blocks(dft_table, data, freq_count, halves)
-    sent = (spectra * LINK_SCALE).astype(jnp.float16)
-    received = lax.all_to_all(sent, "tm", split_axis=0, concat_axis=0, tiled=True)
-    high, low = split_pair(received.astype(jnp.float32))
-    recv_rows = received.shape[0]
-
-    square = gram_call(high, low, weights, 2048, 2 * local_blocks) * (1.0 / (LINK_SCALE * LINK_SCALE * total_points))
+    half_points = points_here // halves
+    chunks = 2
+    width = half_points // chunks
+    pieces = []
+    square = None
+    split_weights = weights.reshape(halves, half_points)
+    for c, spectra in enumerate(transform_blocks(dft_table, data, freq_count, halves, chunks)):
+        sent = (spectra * LINK_SCALE).astype(jnp.float16)
+        received = lax.all_to_all(sent, "tm", split_axis=0, concat_axis=0, tiled=True)
+        high, low = split_pair(received.astype(jnp.float32))
+        pieces.append((high, low))
+        part_weights = split_weights[:, c * width:(c + 1) * width]
+        partial_square = gram_call(high, low, part_weights, width, 2 * local_blocks)
+        square = partial_square if square is None else square + partial_square
+    recv_rows = pieces[0][0].shape[0]
+    square = square * (1.0 / (LINK_SCALE * LINK_SCALE * total_points))
     natural = jnp.arange(rows, dtype=jnp.int32)
     part, block = natural // block_count, natural % block_count
     group = 2 * local_blocks
@@ -203,7 +227,7 @@
     kept_rows = jnp.arange(rows, dtype=jnp.int32) % block_count < kept_count
     coeff = jnp.where(kept_rows[:, None], coeff, jnp.zeros_like(coeff)) * (1.0 / LINK_SCALE)
     coeff_halves = jnp.stack([jnp.dot(coeff, p, precision=HIGH) for p in pick])
-    mode_field = mode_call(coeff_halves, high, low, 2048).reshape(1, 2, block_count, points_here)
+    mode_field = mode_call(coeff_halves, pieces).reshape(1, 2, block_count, points_here)
     energy = (jnp.trace(g_one) / block_count).reshape(1)
     return (mode_field, energy)
 

time: 118 us -> 127 us (1.076)
  starting transfers between devices: 23.1 us -> 33.7 us
  waiting for transfers between devices: 58.5 us -> 52.5 us
  Pallas kernels: 12 us -> 14 us
    all_to_all x1 -> x2, starting transfers between devices: 10.6 us -> 18.8 us  [shards(): lax.all_to_all(sent, 'tm', split_axis=0, concat_axis=0, tiled=True)]
    all_to_all x1 -> x2, waiting for transfers between devices: 48.2 us -> 42.3 us  [shards(): lax.all_to_all(sent, 'tm', split_axis=0, concat_axis=0, tiled=True)]
    all_to_all x1, starting transfers between devices: 12.5 us -> 14.9 us  [shards(): lax.all_to_all(spread, 'space', split_axis=0, concat_axis=0, tiled=True)]
    pallas_call x1 -> x2, Pallas kernels: 5.76 us -> 7.99 us  [gram_call(): pl.pallas_call(functools.partial(gram_kernel, group), grid=(points // chu...]
    dot_general x1 -> x2, matrix products: 2.06 us -> 2.85 us  [transform_blocks(): out.append(jnp.dot(lifted, stacked, preferred_element_type=jnp.float32))]
    convert_element_type x2 -> x3, other arithmetic: 3.49 us -> 4.18 us  [split_pair(): (value - rounded).astype(jnp.bfloat16)]
  transfers between devices with their start and end apart: 2 -> 3, of which waited for: 2 -> 3; matrix products, arithmetic and copies ran while one was open for 2% -> 4% of each run, Pallas kernels for 0% -> 3%
where the time goes in v9:
time: 127 us; the launch traced here: 126 us
  waiting for transfers between devices  52.5 us (41%)
  starting transfers between devices  33.7 us (27%)
  Pallas kernels  14 us (11%)
  other arithmetic  8.49 us (7%)
  matrix products  7.23 us (6%)
  local copies, waits for them, and re-layouts  5.84 us (5%)
  between operations  4.13 us (3%)
    all_to_all x2, waiting for transfers between devices, shards(): lax.all_to_all(sent, 'tm', split_axis=0, concat_axis=0, tiled=True)  42.3 us
    all_to_all x2, starting transfers between devices, shards(): lax.all_to_all(sent, 'tm', split_axis=0, concat_axis=0, tiled=True)  18.8 us
    all_to_all x1, starting transfers between devices, shards(): lax.all_to_all(spread, 'space', split_axis=0, concat_axis=0, tiled=True)  14.9 us
    all_to_all x1, waiting for transfers between devices, shards(): lax.all_to_all(spread, 'space', split_axis=0, concat_axis=0, tiled=True)  10.2 us
    pallas_call x2, Pallas kernels, gram_call(): pl.pallas_call(functools.partial(gram_kernel, group), grid=(points // chu...  7.99 us
    pallas_call x1, Pallas kernels, mode_call(): pl.pallas_call(mode_kernel, grid=(chunks, halves), in_specs=[pl.BlockSpec...  5.98 us
    convert_element_type x3, other arithmetic, split_pair(): (value - rounded).astype(jnp.bfloat16)  4.18 us
    dot_general x2, matrix products, transform_blocks(): out.append(jnp.dot(lifted, stacked, preferred_element_type=jnp.float32))  2.85 us
  transfers between devices with their start and end apart: 3, of which 3 were waited for; matrix products, arithmetic and copies ran while one was open for 4% of the time, Pallas kernels for 3%

profile of v9, /device:TPU:1, one launch (start us, length us, event | category | flops | bytes accessed | tf_op | source)
XLA Modules:
  0.0 125.8 jit_solution(6792706347605443070)
XLA Ops:
  0.6 0.6 multiply_reduce_fusion.1
  2.0 0.8 divide_convert_fusion.1
  2.9 0.1 broadcast_multiply_fusion.1
  3.0 0.3 broadcast_multiply_fusion
  3.3 0.2 mul.187
  3.5 1.7 %fusion.81 = (bf16[128,2048]{1,0:T(8,128)(2,1)S(1)}, bf16[128,2048]{1,0:T(8,128)(2,1)S(1)}, bf16[128,2048]{1,0:T(8,128)(2,1)S(1)}, bf16[128,2048]{1,0:T(8,128)(2,1)S(1)}) fusion(bf16[128,8192]{1,0:T(8,128)(2,1)} %param.4), kind=kLoop, calls=%fused_computation.141 | loop fusion | bytes 4194304 | tf_op jit(solution)/shard_map/slice | solution.py:44
  5.2 1.4 %fusion.2 = f16[32,8,2048]{2,1,0:T(8,128)(2,1)} fusion(bf16[256,256]{1,0:T(8,128)(2,1)S(1)} %mul.187, bf16[128,2048]{1,0:T(8,128)(2,1)S(1)} %get-tuple-element.11, bf16[128,2048]{1,0:T(8,128)(2,1)S(1)} %get-tuple-element.8), kind=kOutput, calls=%fused_computation.8 | convolution fusion | flops 271581184 | bytes 2228224 | tf_op jit(solution)/shard_map/dot_general | solution.py:46
  6.6 10.5 %all-to-all-start.1 = ((f16[32,8,2048]{2,1,0:T(8,128)(2,1)}), f16[32,8,2048]{2,1,0:T(8,128)(2,1)S(1)}, u32[]{:S(2)}, u32[]{:S(2)}) async-start(f16[32,8,2048]{2,1,0:T(8,128)(2,1)} %fusion.2), calls=%async_computation.1 | async-start | bytes 2097152 | tf_op jit(solution)/shard_map/all_to_all | solution.py:180
  17.1 1.4 %fusion.3 = f16[32,8,2048]{2,1,0:T(8,128)(2,1)} fusion(bf16[256,256]{1,0:T(8,128)(2,1)S(1)} %mul.187, bf16[128,2048]{1,0:T(8,128)(2,1)S(1)} %get-tuple-element.9, bf16[128,2048]{1,0:T(8,128)(2,1)S(1)} %get-tuple-element.10), kind=kOutput, calls=%fused_computation.9 | convolution fusion | flops 271581184 | bytes 2228224 | tf_op jit(solution)/shard_map/dot_general | solution.py:46
  18.5 23.4 %all-to-all-done.1 = f16[32,8,2048]{2,1,0:T(8,128)(2,1)S(1)} async-done(((f16[32,8,2048]{2,1,0:T(8,128)(2,1)}), f16[32,8,2048]{2,1,0:T(8,128)(2,1)S(1)}, u32[]{:S(2)}, u32[]{:S(2)}) %all-to-all-start.1) | async-done | bytes 1048608 | tf_op jit(solution)/shard_map/all_to_all | solution.py:180
  42.0 8.3 %all-to-all-start = ((f16[32,8,2048]{2,1,0:T(8,128)(2,1)}), f16[32,8,2048]{2,1,0:T(8,128)(2,1)S(1)}, u32[]{:S(2)}, u32[]{:S(2)}) async-start(f16[32,8,2048]{2,1,0:T(8,128)(2,1)} %fusion.3), calls=%async_computation | async-start | bytes 2097152 | tf_op jit(solution)/shard_map/all_to_all | solution.py:180
  50.4 0.6 fusion.85
  51.0 1.7 %fusion.5 = (bf16[256,2048]{1,0:T(8,128)(2,1)}, bf16[256,2048]{1,0:T(8,128)(2,1)}) fusion(f16[32,8,2048]{2,1,0:T(8,128)(2,1)S(1)} %all-to-all-done.1), kind=kLoop, calls=%fused_computation.11 | loop fusion | flops 2621440 | bytes 3145728 | tf_op jit(solution)/shard_map/convert_element_type | solution.py:52
  52.7 4.0 %shard_map.60 = f32[256,256]{1,0:T(8,128)} custom-call(bf16[256,2048]{1,0:T(8,128)(2,1)} %get-tuple-element.13.hi_ref.refs_2_, bf16[256,2048]{1,0:T(8,128)(2,1)} %get-tuple-element.12.lo_ref.refs_3_, f32[2,2048]{1,0:T(2,128)} %get-tuple-element.40.w_ref), custom_call_target="tpu_custom_call" | custom-call | flops 805306368 | bytes 2097152 | tf_op jit(solution)/shard_map/pallas_call | solution.py:77
  56.7 18.8 %all-to-all-done = f16[32,8,2048]{2,1,0:T(8,128)(2,1)S(1)} async-done(((f16[32,8,2048]{2,1,0:T(8,128)(2,1)}), f16[32,8,2048]{2,1,0:T(8,128)(2,1)S(1)}, u32[]{:S(2)}, u32[]{:S(2)}) %all-to-all-start) | async-done | bytes 1048608 | tf_op jit(solution)/shard_map/all_to_all | solution.py:180
  75.5 1.7 %fusion.4 = (bf16[256,2048]{1,0:T(8,128)(2,1)}, bf16[256,2048]{1,0:T(8,128)(2,1)}) fusion(f16[32,8,2048]{2,1,0:T(8,128)(2,1)S(1)} %all-to-all-done), kind=kLoop, calls=%fused_computation.10 | loop fusion | flops 2621440 | bytes 3145728 | tf_op jit(solution)/shard_map/convert_element_type | solution.py:52
  77.2 4.0 %shard_map.59 = f32[256,256]{1,0:T(8,128)} custom-call(bf16[256,2048]{1,0:T(8,128)(2,1)} %get-tuple-element.15.hi_ref.refs_0_, bf16[256,2048]{1,0:T(8,128)(2,1)} %get-tuple-element.14.lo_ref.refs_1_, f32[2,2048]{1,0:T(2,128)} %get-tuple-element.41.w_ref), custom_call_target="tpu_custom_call" | custom-call | flops 805306368 | bytes 2097152 | tf_op jit(solution)/shard_map/pallas_call | solution.py:77
  81.3 1.3 %fusion.16 = f32[128,256]{1,0:T(8,128)S(1)} fusion(f32[256,256]{1,0:T(8,128)} %shard_map.59, f32[256,256]{1,0:T(8,128)S(1)} %copy-done, s32[256]{0:T(256)S(1)} %and_select_fusion, s32[128]{0:T(128)S(1)} %get-tuple-element.47, s32[128]{0:T(128)S(1)} %get-tuple-element.46), kind=kOutput, calls=%fused_computation.30 | convolution fusion | flops 101089280 | bytes 657408 | tf_op jit(solution)/shard_map/dot_general | solution.py:198
  82.6 0.4 fusion.24
  83.1 0.7 broadcast_in_dim.12
  83.9 14.9 %all-to-all-start.2 = ((f32[16,32,128]{2,1,0:T(8,128)}), f32[16,32,128]{2,1,0:T(8,128)S(1)}, u32[]{:S(2)}, u32[]{:S(2)}) async-start(f32[16,32,128]{2,1,0:T(8,128)} %broadcast_in_dim.12), calls=%async_computation.2 | async-start | bytes 524288 | tf_op jit(solution)/shard_map/all_to_all | solution.py:206
  98.9 0.6 dynamic_slice.3
  99.5 0.7 broadcast_compare_fusion
  100.1 10.2 %all-to-all-done.2 = f32[16,32,128]{2,1,0:T(8,128)S(1)} async-done(((f32[16,32,128]{2,1,0:T(8,128)}), f32[16,32,128]{2,1,0:T(8,128)S(1)}, u32[]{:S(2)}, u32[]{:S(2)}) %all-to-all-start.2) | async-done | bytes 262176 | tf_op jit(solution)/shard_map/all_to_all | solution.py:206
  110.4 0.1 copy.36
  110.6 0.1 copy.48
  110.7 0.1 copy.47
  110.8 0.1 copy.46
  110.9 0.1 copy.45
  111.0 0.1 copy.44
  111.1 0.1 copy.43
  111.2 0.1 copy.42
  111.9 0.1 copy.50
  112.4 0.6 select_reduce_fusion
  113.0 0.7 multiply_reduce_fusion
  114.4 0.3 fusion.33
  114.7 0.3 fusion.8
  115.0 0.3 fusion.32
  115.3 0.2 fusion.86
  115.5 0.2 fusion.7
  115.7 0.2 fusion.87
  115.9 0.2 fusion.88
  116.1 0.2 fusion.6
  116.3 0.3 fusion.89
  116.8 0.3 convolution_bitcast_fusion.1
  117.1 0.3 convolution_bitcast_fusion
  118.0 0.7 fusion.15
  118.7 6.0 %shard_map.61 = bf16[128,8192]{1,0:T(8,128)(2,1)} custom-call(bf16[2,128,256]{2,1,0:T(8,128)(2,1)} %get-tuple-element.17.c_hi_ref, bf16[2,128,256]{2,1,0:T(8,128)(2,1)} %get-tuple-element.16.c_lo_ref, bf16[256,2048]{1,0:T(8,128)(2,1)} %get-tuple-element.15.hi_ref.refs_0_, bf16[256,2048]{1,0:T(8,128)(2,1)} %get-tuple-element.14.lo_ref.refs_1_, ...), custom_call_target="tpu_custom_call" | custom-call | flops 1610612736 | bytes 6291456 | tf_op jit(solution)/shard_map/pallas_call | solution.py:118
  (36 shorter events, 1.6 us)
Async XLA Ops:
  6.6 35.4 %all-to-all-start.1 = ((f16[32,8,2048]{2,1,0:T(8,128)(2,1)}), f16[32,8,2048]{2,1,0:T(8,128)(2,1)S(1)}, u32[]{:S(2)}, u32[]{:S(2)}) async-start(f16[32,8,2048]{2,1,0:T(8,128)(2,1)} %fusion.2), calls=%async_computation.1 | async-start | bytes 2097152 | tf_op jit(solution)/shard_map/all_to_all | solution.py:180
  17.1 33.2 %copy-start.1 = (f32[8192]{0:T(1024)S(1)}, f32[8192]{0:T(1024)}, u32[]{:S(2)}) copy-start(f32[8192]{0:T(1024)} %param.5) | copy-start | bytes 98308
  42.0 33.5 %all-to-all-start = ((f16[32,8,2048]{2,1,0:T(8,128)(2,1)}), f16[32,8,2048]{2,1,0:T(8,128)(2,1)S(1)}, u32[]{:S(2)}, u32[]{:S(2)}) async-start(f16[32,8,2048]{2,1,0:T(8,128)(2,1)} %fusion.3), calls=%async_computation | async-start | bytes 2097152 | tf_op jit(solution)/shard_map/all_to_all | solution.py:180
  77.2 4.0 %copy-start = (f32[256,256]{1,0:T(8,128)S(1)}, f32[256,256]{1,0:T(8,128)}, u32[]{:S(2)}) copy-start(f32[256,256]{1,0:T(8,128)} %shard_map.60) | copy-start | bytes 786436
  77.2 21.6 %copy-start.2 = (s32[32]{0:T(128)S(1)}, s32[32]{0:T(128)}, u32[]{:S(2)}) copy-start(s32[32]{0:T(128)} %param.7) | copy-start | bytes 388
  83.9 26.5 %all-to-all-start.2 = ((f32[16,32,128]{2,1,0:T(8,128)}), f32[16,32,128]{2,1,0:T(8,128)S(1)}, u32[]{:S(2)}, u32[]{:S(2)}) async-start(f32[16,32,128]{2,1,0:T(8,128)} %broadcast_in_dim.12), calls=%async_computation.2 | async-start | bytes 524288 | tf_op jit(solution)/shard_map/all_to_all | solution.py:206
